TPU v7x, 32 devices: a whole 2x2x4 slice. The times are simulated.
32 devices in a mesh: src: 8 (over z, x), tgt: 4 (over y, core).
Axes of the slice: x: 2, y: 2, z: 4, core: 2. Of those that a mesh axis runs over, the one named last changes fastest.
Arguments:
- src_emb: bfloat16 [64, 16384], P(None, 'src'), may hold values from -2.75 to 2.75
- tgt_emb: bfloat16 [64, 32768], P(None, 'tgt'), may hold values from -2.75 to 2.75
- target_features: bfloat16 [128, 32768], P(None, 'tgt'), may hold values from -6 to 6
- src_mass: float32 [16384], P('src'), may hold values from 1 to 10
- tgt_mass: float32 [32768], P('tgt'), may hold values from 1 to 10
- kept_blocks: int32 [64, 32], P('src', 'tgt'), may hold values from 0 to 31, as said below
- kept_count: int32 [64, 4], P('src', 'tgt'), may hold values from 1 to 8
Outputs:
- projected: float32 [16384, 128], P(('src', 'tgt'))
- src_potential: float32 [16384], P('src')
- tgt_potential: float32 [32768], P('tgt')
Inputs may be any that keep to these rules, and one draw needn't show every extreme that they name: `kept_blocks`: entry [r, t * 8 + k] is a block number within target shard t; the 8 entries of one group are distinct; the first kept_count[r, t] of them are kept, the others are unused; every target block is kept by some source block row.
All inputs are finite; a program needn't handle non-finite values.
Results may differ from a plain program's by a relative error of at most 0.00075.
Values sent between devices are 32-bit elements; how exact they have to be, the bound alone decides.
No kernel may reach another device: no remote copies, remote signals or barrier semaphores. Data moves between devices by JAX's collectives and lax.ppermute only.
A program may use at most 64 MiB of HBM per device.

v0:
```python
import functools

import jax
import jax.numpy as jnp
from jax import lax
from jax.experimental import pallas as pl
from jax.experimental.pallas import tpu as pltpu
from jax.sharding import PartitionSpec as P

BLOCK = 256
ITERS = 2


SENTINEL = -1e30
EPSILON = 0.1
SCALE = 1.0 / EPSILON


def lse_pair(top, total, other_top, other_total):
    overall = jnp.maximum(top, other_top)
    return (overall, total * jnp.exp(top - overall) + other_total * jnp.exp(other_top - overall))


def butterfly_lse(highest, totals, axis):
    size = lax.axis_size(axis)
    step = 1
    while step < size:
        pairs = [(i, i ^ step) for i in range(size)]
        other = lax.ppermute(jnp.stack([highest, totals]), axis, pairs)
        highest, totals = lse_pair(highest, totals, other[0], other[1])
        step *= 2
    return (highest, totals)


def halving_merge(top, numerator, denominator, axis):
    size = lax.axis_size(axis)
    me = lax.axis_index(axis)
    rows = top.shape[0] // size
    top = top.reshape(size, rows)
    denominator = denominator.reshape(size, rows)
    numerator = numerator.reshape(size, rows, numerator.shape[-1])
    step = 1
    while step < size:
        pairs = [(i, i ^ step) for i in range(size)]
        keep = (me // step) % 2
        count = top.shape[0] // 2

        def split(x):
            x = x.reshape((count, 2) + x.shape[1:])
            return (
                lax.dynamic_index_in_dim(x, keep, axis=1, keepdims=False),
                lax.dynamic_index_in_dim(x, 1 - keep, axis=1, keepdims=False),
            )

        top_keep, top_send = split(top)
        den_keep, den_send = split(denominator)
        num_keep, num_send = split(numerator)
        small = lax.ppermute(jnp.stack([top_send, den_send]), axis, pairs)
        num_other = lax.ppermute(num_send, axis, pairs)
        overall = jnp.maximum(top_keep, small[0])
        mine = jnp.exp(top_keep - overall)
        theirs = jnp.exp(small[0] - overall)
        numerator = num_keep * mine[..., None] + num_other * theirs[..., None]
        denominator = den_keep * mine + small[1] * theirs
        top = overall
        step *= 2
    return (numerator.reshape(rows, -1), denominator.reshape(rows))


CHUNK = 64


def tile_slice(ref, b):
    return ref[:, pl.ds(pl.multiple_of(b * BLOCK, BLOCK), BLOCK)]


def doubled_source(src_ref):
    exact = src_ref[...].astype(jnp.float32)
    return (exact * 2.0).astype(jnp.bfloat16), jnp.sum(exact * exact, axis=1, keepdims=True)


def as_row(column, scratch):
    scratch[...] = jnp.broadcast_to(column, scratch.shape)
    return jnp.transpose(scratch[...])[0:1, :]


def as_column(row, scratch):
    scratch[...] = jnp.broadcast_to(row, scratch.shape)
    return jnp.transpose(scratch[...])[:, 0:1]


def by_count(live, slots, body):
    for count in range(1, slots + 1):
        pl.when(live == count)(functools.partial(body, count))


def fill_shifted(blocks_ref, r, count, doubled, tgt_ref, tnorm_ref, tpot_ref, held):
    for k in range(count):
        b = blocks_ref[r, k]
        shift = tile_slice(tpot_ref, b) - tile_slice(tnorm_ref, b)
        held[k] = jnp.dot(doubled, tile_slice(tgt_ref, b), preferred_element_type=jnp.float32) + shift


def chunk_peak(held, count, rows):
    peak = held[0, rows, :]
    for k in range(1, count):
        peak = jnp.maximum(peak, held[k, rows, :])
    return jnp.max(peak, axis=1, keepdims=True)


def row_kernel(blocks_ref, count_ref, src_ref, tgt_ref, tnorm_ref, tpot_ref,
               high_ref, total_ref, held, high_col, total_col, wide):
    r = pl.program_id(0)
    doubled, snorm = doubled_source(src_ref)

    def body(count):
        fill_shifted(blocks_ref, r, count, doubled, tgt_ref, tnorm_ref, tpot_ref, held)
        for chunk in range(BLOCK // CHUNK):
            rows = pl.ds(chunk * CHUNK, CHUNK)
            peak = chunk_peak(held, count, rows)
            acc = jnp.exp((held[0, rows, :] - peak) * SCALE)
            for k in range(1, count):
                acc = acc + jnp.exp((held[k, rows, :] - peak) * SCALE)
            high_col[rows, :] = peak
            total_col[rows, :] = jnp.sum(acc, axis=1, keepdims=True)

    by_count(count_ref[r, 0], held.shape[0], body)
    high_ref[...] = as_row((high_col[...] - snorm) * SCALE, wide)
    total_ref[...] = as_row(total_col[...], wide)


def column_kernel(blocks_ref, count_ref, src_ref, spot_ref, tgt_ref, tnorm_ref,
                  top_ref, sum_ref, tall):
    r = pl.program_id(0)

    @pl.when(r == 0)
    def _():
        top_ref[...] = jnp.full(top_ref.shape, SENTINEL, jnp.float32)
        sum_ref[...] = jnp.zeros(sum_ref.shape, jnp.float32)

    doubled, snorm = doubled_source(src_ref)
    shift = as_column(spot_ref[...], tall) - snorm

    def body(count):
        for k in range(count):
            b = blocks_ref[r, k]
            lanes = pl.ds(pl.multiple_of(b * BLOCK, BLOCK), BLOCK)
            shifted = jnp.dot(doubled, tile_slice(tgt_ref, b),
                              preferred_element_type=jnp.float32) + shift
            peak = jnp.max(shifted, axis=0, keepdims=True)
            totals = jnp.sum(jnp.exp((shifted - peak) * SCALE), axis=0, keepdims=True)
            highest = (peak - tnorm_ref[:, lanes]) * SCALE
            old_top = top_ref[:, lanes]
            new_top = jnp.maximum(old_top, highest)
            sum_ref[:, lanes] = (sum_ref[:, lanes] * jnp.exp(old_top - new_top)
                                 + totals * jnp.exp(highest - new_top))
            top_ref[:, lanes] = new_top

    by_count(count_ref[r, 0], blocks_ref.shape[1], body)


def project_kernel(blocks_ref, count_ref, src_ref, tgt_ref, tnorm_ref, tpot_ref, feat_ref,
                   top_ref, num_ref, den_ref, held, weights, high_col, den_col, wide):
    r = pl.program_id(0)
    doubled, snorm = doubled_source(src_ref)

    def body(count):
        fill_shifted(blocks_ref, r, count, doubled, tgt_ref, tnorm_ref, tpot_ref, held)
        for chunk in range(BLOCK // CHUNK):
            rows = pl.ds(chunk * CHUNK, CHUNK)
            peak = chunk_peak(held, count, rows)
            acc = jnp.zeros((CHUNK, BLOCK), jnp.float32)
            for k in range(count):
                rounded = jnp.exp((held[k, rows, :] - peak) * SCALE).astype(jnp.bfloat16)
                weights[k, rows, :] = rounded
                acc = acc + rounded.astype(jnp.float32)
            high_col[rows, :] = peak
            den_col[rows, :] = jnp.sum(acc, axis=1, keepdims=True)
        total = None
        for k in range(count):
            part = lax.dot_general(weights[k], tile_slice(feat_ref, blocks_ref[r, k]),
                                   (((1,), (1,)), ((), ())), preferred_element_type=jnp.float32)
            total = part if total is None else total + part
        num_ref[...] = total

    by_count(count_ref[r, 0], held.shape[0], body)
    top_ref[...] = as_row((high_col[...] - snorm) * SCALE, wide)
    den_ref[...] = as_row(den_col[...], wide)


def whole(shape):
    return pl.BlockSpec(shape, lambda r, *_: (0,) * len(shape))


def per_row(width):
    return pl.BlockSpec((BLOCK, width), lambda r, *_: (r, 0))


def lane_row():
    return pl.BlockSpec((1, BLOCK), lambda r, *_: (0, r))


def column_scratch():
    return pltpu.VMEM((BLOCK, 1), jnp.float32)


def row_pass(blocks, counts, src_t, tgt, tnorm, tpot):
    rows = src_t.shape[0]
    slots = blocks.shape[1]
    spec = pltpu.PrefetchScalarGridSpec(
        num_scalar_prefetch=2,
        grid=(rows // BLOCK,),
        in_specs=[per_row(src_t.shape[1]), whole(tgt.shape), whole(tnorm.shape), whole(tpot.shape)],
        out_specs=[lane_row(), lane_row()],
        scratch_shapes=[pltpu.VMEM((slots, BLOCK, BLOCK), jnp.float32), column_scratch(),
                        column_scratch(), pltpu.VMEM((BLOCK, 128), jnp.float32)],
    )
    return pl.pallas_call(
        row_kernel,
        grid_spec=spec,
        out_shape=[jax.ShapeDtypeStruct((1, rows), jnp.float32)] * 2,
        compiler_params=pltpu.CompilerParams(dimension_semantics=("arbitrary",)),
    )(blocks, counts, src_t, tgt, tnorm, tpot)


def column_pass(blocks, counts, src_t, spot, tgt, tnorm):
    rows = src_t.shape[0]
    spec = pltpu.PrefetchScalarGridSpec(
        num_scalar_prefetch=2,
        grid=(rows // BLOCK,),
        in_specs=[per_row(src_t.shape[1]), lane_row(), whole(tgt.shape), whole(tnorm.shape)],
        out_specs=[whole(tnorm.shape), whole(tnorm.shape)],
        scratch_shapes=[pltpu.VMEM((128, BLOCK), jnp.float32)],
    )
    return pl.pallas_call(
        column_kernel,
        grid_spec=spec,
        out_shape=[jax.ShapeDtypeStruct(tnorm.shape, jnp.float32)] * 2,
        compiler_params=pltpu.CompilerParams(dimension_semantics=("arbitrary",)),
    )(blocks, counts, src_t, spot, tgt, tnorm)


def project_pass(blocks, counts, src_t, tgt, tnorm, tpot, feat):
    rows = src_t.shape[0]
    slots = blocks.shape[1]
    feats = feat.shape[0]
    spec = pltpu.PrefetchScalarGridSpec(
        num_scalar_prefetch=2,
        grid=(rows // BLOCK,),
        in_specs=[per_row(src_t.shape[1]), whole(tgt.shape), whole(tnorm.shape),
                  whole(tpot.shape), whole(feat.shape)],
        out_specs=[lane_row(), per_row(feats), lane_row()],
        scratch_shapes=[pltpu.VMEM((slots, BLOCK, BLOCK), jnp.float32),
                        pltpu.VMEM((slots, BLOCK, BLOCK), jnp.bfloat16),
                        column_scratch(), column_scratch(), pltpu.VMEM((BLOCK, 128), jnp.float32)],
    )
    return pl.pallas_call(
        project_kernel,
        grid_spec=spec,
        out_shape=[jax.ShapeDtypeStruct((1, rows), jnp.float32),
                   jax.ShapeDtypeStruct((rows, feats), jnp.float32),
                   jax.ShapeDtypeStruct((1, rows), jnp.float32)],
        compiler_params=pltpu.CompilerParams(dimension_semantics=("arbitrary",)),
    )(blocks, counts, src_t, tgt, tnorm, tpot, feat)


def shards(src_emb, tgt_emb, target_features, src_mass, tgt_mass, kept_blocks, kept_count):
    src_rows = src_emb.shape[1]
    tgt_rows = tgt_emb.shape[1]
    src_t = src_emb.T
    tnorm = jnp.sum(jnp.square(tgt_emb.astype(jnp.float32)), axis=0).reshape(1, tgt_rows)
    counts = kept_count.reshape(-1, 1)

    tgt_potential = jnp.zeros((tgt_rows,), jnp.float32)
    src_potential = jnp.zeros((src_rows,), jnp.float32)
    for iteration in range(ITERS):
        tpot = tgt_potential.reshape(1, tgt_rows)
        highest, totals = row_pass(kept_blocks, counts, src_t, tgt_emb, tnorm, tpot)
        highest, totals = butterfly_lse(highest.reshape(src_rows), totals.reshape(src_rows), "tgt")
        src_potential = EPSILON * jnp.log(src_mass) - EPSILON * (highest + jnp.log(totals))
        block_top, block_sum = column_pass(
            kept_blocks, counts, src_t, src_potential.reshape(1, src_rows), tgt_emb, tnorm
        )
        block_top, block_sum = butterfly_lse(
            block_top.reshape(tgt_rows), block_sum.reshape(tgt_rows), "src"
        )
        tgt_potential = EPSILON * jnp.log(tgt_mass) - EPSILON * (block_top + jnp.log(block_sum))

    tpot = tgt_potential.reshape(1, tgt_rows)
    local_top, numerator, denominator = project_pass(
        kept_blocks, counts, src_t, tgt_emb, tnorm, tpot, target_features
    )
    numerator, denominator = halving_merge(
        local_top.reshape(src_rows), numerator, denominator.reshape(src_rows), "tgt"
    )
    projected = numerator / denominator[:, None]
    return (projected, src_potential, tgt_potential)


def solution(mesh):
    return jax.shard_map(
        shards,
        mesh=mesh,
        in_specs=(
            P(None, "src"),
            P(None, "tgt"),
            P(None, "tgt"),
            P("src"),
            P("tgt"),
            P("src", "tgt"),
            P("src", "tgt"),
        ),
        out_specs=(P(("src", "tgt"), None), P("src"), P("tgt")),
        check_vma=False,
    )
```

profile of v0, /device:TPU:0, one launch (start us, length us, event | category | flops | bytes accessed | tf_op | source)
XLA Modules:
  0.0 136.3 jit_solution(7691251178999028465)
XLA Ops:
  2.0 2.1 %multiply_reduce_fusion = f32[8192]{0:T(1024)} fusion(bf16[64,8192]{1,0:T(8,128)(2,1)} %tgt_ref.9), kind=kLoop, calls=%fused_computation | loop fusion | flops 1564672 | bytes 1081344 | tf_op jit(solution)/shard_map/reduce_sum | solution.py:271
  4.1 2.0 %copy.10 = bf16[64,2048]{0,1:T(8,128)(2,1)} copy(bf16[64,2048]{1,0:T(8,128)(2,1)} %param.7) | data formatting | bytes 524288 | tf_op args[0]
  6.7 11.1 %shard_map.94 = (f32[1,2048]{1,0:T(1,128)}, f32[1,2048]{1,0:T(1,128)}) custom-call(s32[8,8]{1,0:T(8,128)} %blocks_ref.9, s32[8,1]{1,0:T(8,128)} %copy.15.count_ref, bf16[2048,64]{1,0:T(8,128)(2,1)} %bitcast.95, bf16[64,8192]{1,0:T(8,128)(2,1)} %tgt_ref.9, f32[1,8192]{1,0:T(1,128)} %bitcast.100, f32[1,8192]{1,0:T(1,128)} %reshape.107.tpot_ref), custom_call_target="tpu_custom_call" | custom-call | tf_op jit(solution)/shard_map/pallas_call | solution.py:218
  21.1 2.1 %collective-permute-start.1 = (f32[2,2048]{1,0:T(2,128)S(1)}, f32[2,2048]{1,0:T(2,128)S(1)}, u32[]{:S(2)}, u32[]{:S(2)}) collective-permute-start(f32[2,2048]{1,0:T(2,128)S(1)} %pad_maximum_fusion.7), channel_id=1, source_target_pairs={{0,2},{1,3},{2,0},{3,1},{4,6},{5,7},{6,4},{7,5},{8,10},{9,11},{10,... | collective-permute-start | bytes 49160 | tf_op jit(solution)/shard_map/ppermute | solution.py:29
  23.2 1.7 %collective-permute-done.1 = f32[2,2048]{1,0:T(2,128)S(1)} collective-permute-done((f32[2,2048]{1,0:T(2,128)S(1)}, f32[2,2048]{1,0:T(2,128)S(1)}, u32[]{:S(2)}, u32[]{:S(2)}) %collective-permute-start.1) | collective-permute-done | bytes 16416 | tf_op jit(solution)/shard_map/ppermute | solution.py:29
  26.3 10.0 %shard_map.95 = (f32[1,8192]{1,0:T(1,128)}, f32[1,8192]{1,0:T(1,128)}) custom-call(s32[8,8]{1,0:T(8,128)} %blocks_ref.9, s32[8,1]{1,0:T(8,128)} %copy.15.count_ref, bf16[2048,64]{1,0:T(8,128)(2,1)} %bitcast.96, f32[1,2048]{1,0:T(1,128)} %bitcast.130, bf16[64,8192]{1,0:T(8,128)(2,1)} %tgt_ref.9, f32[1,8192]{1,0:T(1,128)} %bitcast.101), custom_call_target="tpu_custom_call" | custom-call | tf_op jit(solution)/shard_map/pallas_call | solution.py:235
  37.2 4.3 %collective-permute-done.2 = f32[2,8192]{1,0:T(2,128)S(1)} collective-permute-done((f32[2,8192]{1,0:T(2,128)S(1)}, f32[2,8192]{1,0:T(2,128)S(1)}, u32[]{:S(2)}, u32[]{:S(2)}) %collective-permute-start.2) | collective-permute-done | bytes 65568 | tf_op jit(solution)/shard_map/ppermute | solution.py:29
  43.3 3.5 %collective-permute-done.3 = f32[2,8192]{1,0:T(2,128)S(1)} collective-permute-done((f32[2,8192]{1,0:T(2,128)S(1)}, f32[2,8192]{1,0:T(2,128)S(1)}, u32[]{:S(2)}, u32[]{:S(2)}) %collective-permute-start.3) | collective-permute-done | bytes 65568 | tf_op jit(solution)/shard_map/ppermute | solution.py:29
  47.0 4.4 %collective-permute-start.4 = (f32[2,8192]{1,0:T(2,128)S(1)}, f32[2,8192]{1,0:T(2,128)S(1)}, u32[]{:S(2)}, u32[]{:S(2)}) collective-permute-start(f32[2,8192]{1,0:T(2,128)S(1)} %pad_maximum_fusion.2), channel_id=1, source_target_pairs={{0,16},{4,20},{8,24},{12,28},{16,0},{20,4},{24,8},{28,12},{1,17},{... | collective-permute-start | bytes 196616 | tf_op jit(solution)/shard_map/ppermute | solution.py:29
  51.4 2.4 %collective-permute-done.4 = f32[2,8192]{1,0:T(2,128)S(1)} collective-permute-done((f32[2,8192]{1,0:T(2,128)S(1)}, f32[2,8192]{1,0:T(2,128)S(1)}, u32[]{:S(2)}, u32[]{:S(2)}) %collective-permute-start.4) | collective-permute-done | bytes 65568 | tf_op jit(solution)/shard_map/ppermute | solution.py:29
  53.8 1.5 %multiply_subtract_fusion.1 = f32[8192]{0:T(1024)} fusion(f32[8192]{0:T(1024)S(1)} %bitcast.114, f32[8192]{0:T(1024)S(1)} %bitcast.113, f32[8192]{0:T(1024)S(1)} %bitcast.124, f32[8192]{0:T(1024)S(1)} %bitcast.123, f32[8192]{0:T(1024)S(1)} %bitcast.122, f32[8192]{0:T(1024)S(1)} %bitcast.121, f32[8192]{0:T(1024)} %bitcast.109, f32[8192]{0:T(1024)} %bitcast.110, ...), kind=kLoop, calls=%fused_computation.23 | loop fusion | flops 180224 | bytes 327680 | tf_op jit(solution)/shard_map/sub | solution.py:287
  55.3 11.1 %shard_map.96 = (f32[1,2048]{1,0:T(1,128)}, f32[1,2048]{1,0:T(1,128)}) custom-call(s32[8,8]{1,0:T(8,128)} %blocks_ref.9, s32[8,1]{1,0:T(8,128)} %copy.15.count_ref, bf16[2048,64]{1,0:T(8,128)(2,1)} %bitcast.97, bf16[64,8192]{1,0:T(8,128)(2,1)} %tgt_ref.9, f32[1,8192]{1,0:T(1,128)} %bitcast.102, f32[1,8192]{1,0:T(1,128)} %bitcast.112), custom_call_target="tpu_custom_call" | custom-call | tf_op jit(solution)/shard_map/pallas_call | solution.py:218
  69.3 3.6 %collective-permute-done.6 = f32[2,2048]{1,0:T(2,128)S(1)} collective-permute-done((f32[2,2048]{1,0:T(2,128)S(1)}, f32[2,2048]{1,0:T(2,128)S(1)}, u32[]{:S(2)}, u32[]{:S(2)}) %collective-permute-start.6) | collective-permute-done | bytes 16416 | tf_op jit(solution)/shard_map/ppermute | solution.py:29
  74.3 10.0 %shard_map.97 = (f32[1,8192]{1,0:T(1,128)}, f32[1,8192]{1,0:T(1,128)}) custom-call(s32[8,8]{1,0:T(8,128)} %blocks_ref.9, s32[8,1]{1,0:T(8,128)} %copy.15.count_ref, bf16[2048,64]{1,0:T(8,128)(2,1)} %bitcast.98, f32[1,2048]{1,0:T(1,128)} %bitcast.129, bf16[64,8192]{1,0:T(8,128)(2,1)} %tgt_ref.9, f32[1,8192]{1,0:T(1,128)} %bitcast.103), custom_call_target="tpu_custom_call" | custom-call | tf_op jit(solution)/shard_map/pallas_call | solution.py:235
  85.2 4.3 %collective-permute-done.7 = f32[2,8192]{1,0:T(2,128)S(1)} collective-permute-done((f32[2,8192]{1,0:T(2,128)S(1)}, f32[2,8192]{1,0:T(2,128)S(1)}, u32[]{:S(2)}, u32[]{:S(2)}) %collective-permute-start.7) | collective-permute-done | bytes 65568 | tf_op jit(solution)/shard_map/ppermute | solution.py:29
  90.5 4.3 %collective-permute-done.8 = f32[2,8192]{1,0:T(2,128)S(1)} collective-permute-done((f32[2,8192]{1,0:T(2,128)S(1)}, f32[2,8192]{1,0:T(2,128)S(1)}, u32[]{:S(2)}, u32[]{:S(2)}) %collective-permute-start.8) | collective-permute-done | bytes 65568 | tf_op jit(solution)/shard_map/ppermute | solution.py:29
  95.0 4.3 %collective-permute-start.9 = (f32[2,8192]{1,0:T(2,128)S(1)}, f32[2,8192]{1,0:T(2,128)S(1)}, u32[]{:S(2)}, u32[]{:S(2)}) collective-permute-start(f32[2,8192]{1,0:T(2,128)S(1)} %pad_maximum_fusion.5), channel_id=1, source_target_pairs={{0,16},{4,20},{8,24},{12,28},{16,0},{20,4},{24,8},{28,12},{1,17},{... | collective-permute-start | bytes 196616 | tf_op jit(solution)/shard_map/ppermute | solution.py:29
  99.3 2.4 %collective-permute-done.9 = f32[2,8192]{1,0:T(2,128)S(1)} collective-permute-done((f32[2,8192]{1,0:T(2,128)S(1)}, f32[2,8192]{1,0:T(2,128)S(1)}, u32[]{:S(2)}, u32[]{:S(2)}) %collective-permute-start.9) | collective-permute-done | bytes 65568 | tf_op jit(solution)/shard_map/ppermute | solution.py:29
  101.7 1.5 %multiply_subtract_fusion = f32[8192]{0:T(1024)} fusion(f32[8192]{0:T(1024)S(1)} %bitcast.116, f32[8192]{0:T(1024)S(1)} %bitcast.115, f32[8192]{0:T(1024)S(1)} %bitcast.120, f32[8192]{0:T(1024)S(1)} %bitcast.119, f32[8192]{0:T(1024)S(1)} %bitcast.118, f32[8192]{0:T(1024)S(1)} %bitcast.117, f32[8192]{0:T(1024)} %bitcast.107, f32[8192]{0:T(1024)} %bitcast.108, ...), kind=kLoop, calls=%fused_computation.11 | loop fusion | flops 180224 | bytes 327680 | tf_op jit(solution)/shard_map/sub | solution.py:287
  103.2 15.7 %shard_map.98 = (f32[1,2048]{1,0:T(1,128)}, f32[2048,128]{1,0:T(8,128)}, f32[1,2048]{1,0:T(1,128)}) custom-call(s32[8,8]{1,0:T(8,128)} %blocks_ref.9, s32[8,1]{1,0:T(8,128)} %copy.15.count_ref, bf16[2048,64]{1,0:T(8,128)(2,1)} %bitcast.99, bf16[64,8192]{1,0:T(8,128)(2,1)} %tgt_ref.9, f32[1,8192]{1,0:T(1,128)} %bitcast.104, f32[1,8192]{1,0:T(1,128)} %bitcast.111, ...), custom_call_target="tpu_custom_call" | custom-call | tf_op jit(solution)/shard_map/pallas_call | solution.py:257
  123.9 1.4 %collective-permute-done.10 = f32[2,2,512]{2,1,0:T(2,128)S(1)} collective-permute-done((f32[2,2,512]{2,1,0:T(2,128)S(1)}, f32[2,2,512]{2,1,0:T(2,128)S(1)}, u32[]{:S(2)}, u32[]{:S(2)}) %collective-permute-start.10) | collective-permute-done | bytes 8224 | tf_op jit(solution)/shard_map/ppermute | solution.py:58
  125.3 1.4 %fusion = f32[2,512,128]{2,1,0:T(8,128)S(1)} fusion(f32[2,512,128]{2,1,0:T(8,128)S(1)} %collective-permute-done.11, f32[2,2,512,128]{3,2,1,0:T(8,128)} %bitcast.106, s32[]{:T(128)S(6)} %select_n.41, f32[2,512]{1,0:T(2,128)S(1)} %get-tuple-element.30, f32[2,512]{1,0:T(2,128)S(1)} %get-tuple-element.29), kind=kLoop, calls=%fused_computation.2 | loop fusion | flops 393216 | bytes 1581060 | tf_op jit(solution)/shard_map/add | solution.py:63
  126.8 2.0 %collective-permute-start.12 = (f32[2,1,512]{2,1,0:T(1,128)S(1)}, f32[2,1,512]{2,1,0:T(1,128)S(1)}, u32[]{:S(2)}, u32[]{:S(2)}) collective-permute-start(f32[2,1,512]{2,1,0:T(1,128)S(1)} %pad_maximum_fusion.11), channel_id=1, source_target_pairs={{0,2},{1,3},{2,0},{3,1},{4,6},{5,7},{6,4},{7,5},{8,10},{9,11},{10,... | collective-permute-start | bytes 12296 | tf_op jit(solution)/shard_map/ppermute | solution.py:58
  128.9 6.4 %collective-permute-done.12 = f32[2,1,512]{2,1,0:T(1,128)S(1)} collective-permute-done((f32[2,1,512]{2,1,0:T(1,128)S(1)}, f32[2,1,512]{2,1,0:T(1,128)S(1)}, u32[]{:S(2)}, u32[]{:S(2)}) %collective-permute-start.12) | collective-permute-done | bytes 4128 | tf_op jit(solution)/shard_map/ppermute | solution.py:58
  (59 shorter events, 22.2 us)
Async XLA Ops:
  0.6 24.3 %copy-start.1 = (f32[2048]{0:T(1024)S(1)}, f32[2048]{0:T(1024)}, u32[]{:S(2)}) copy-start(f32[2048]{0:T(1024)} %param.10) | copy-start | bytes 24580
  6.7 47.2 %copy-start = (f32[8192]{0:T(1024)S(1)}, f32[8192]{0:T(1024)}, u32[]{:S(2)}) copy-start(f32[8192]{0:T(1024)} %param.11) | copy-start | bytes 98308
  18.5 1.8 %collective-permute-start = (f32[2,2048]{1,0:T(2,128)S(1)}, f32[2,2048]{1,0:T(2,128)S(1)}, u32[]{:S(2)}, u32[]{:S(2)}) collective-permute-start(f32[2,2048]{1,0:T(2,128)S(1)} %pad_maximum_fusion.6), channel_id=1, source_target_pairs={{0,1},{1,0},{2,3},{3,2},{4,5},{5,4},{6,7},{7,6},{8,9},{9,8},{10,11... | collective-permute-start | bytes 49160 | tf_op jit(solution)/shard_map/ppermute | solution.py:29
  21.1 3.8 %collective-permute-start.1 = (f32[2,2048]{1,0:T(2,128)S(1)}, f32[2,2048]{1,0:T(2,128)S(1)}, u32[]{:S(2)}, u32[]{:S(2)}) collective-permute-start(f32[2,2048]{1,0:T(2,128)S(1)} %pad_maximum_fusion.7), channel_id=1, source_target_pairs={{0,2},{1,3},{2,0},{3,1},{4,6},{5,7},{6,4},{7,5},{8,10},{9,11},{10,... | collective-permute-start | bytes 49160 | tf_op jit(solution)/shard_map/ppermute | solution.py:29
  37.1 4.3 %collective-permute-start.2 = (f32[2,8192]{1,0:T(2,128)S(1)}, f32[2,8192]{1,0:T(2,128)S(1)}, u32[]{:S(2)}, u32[]{:S(2)}) collective-permute-start(f32[2,8192]{1,0:T(2,128)S(1)} %pad_maximum_fusion), channel_id=1, source_target_pairs={{0,4},{4,0},{8,12},{12,8},{16,20},{20,16},{24,28},{28,24},{1,5},{5... | collective-permute-start | bytes 196616 | tf_op jit(solution)/shard_map/ppermute | solution.py:29
  42.4 4.3 %collective-permute-start.3 = (f32[2,8192]{1,0:T(2,128)S(1)}, f32[2,8192]{1,0:T(2,128)S(1)}, u32[]{:S(2)}, u32[]{:S(2)}) collective-permute-start(f32[2,8192]{1,0:T(2,128)S(1)} %pad_maximum_fusion.1), channel_id=1, source_target_pairs={{0,8},{4,12},{8,0},{12,4},{16,24},{20,28},{24,16},{28,20},{1,9},{5... | collective-permute-start | bytes 196616 | tf_op jit(solution)/shard_map/ppermute | solution.py:29
  47.0 6.8 %collective-permute-start.4 = (f32[2,8192]{1,0:T(2,128)S(1)}, f32[2,8192]{1,0:T(2,128)S(1)}, u32[]{:S(2)}, u32[]{:S(2)}) collective-permute-start(f32[2,8192]{1,0:T(2,128)S(1)} %pad_maximum_fusion.2), channel_id=1, source_target_pairs={{0,16},{4,20},{8,24},{12,28},{16,0},{20,4},{24,8},{28,12},{1,17},{... | collective-permute-start | bytes 196616 | tf_op jit(solution)/shard_map/ppermute | solution.py:29
  67.1 1.2 collective-permute-start.5
  69.2 3.8 %collective-permute-start.6 = (f32[2,2048]{1,0:T(2,128)S(1)}, f32[2,2048]{1,0:T(2,128)S(1)}, u32[]{:S(2)}, u32[]{:S(2)}) collective-permute-start(f32[2,2048]{1,0:T(2,128)S(1)} %pad_maximum_fusion.9), channel_id=1, source_target_pairs={{0,2},{1,3},{2,0},{3,1},{4,6},{5,7},{6,4},{7,5},{8,10},{9,11},{10,... | collective-permute-start | bytes 49160 | tf_op jit(solution)/shard_map/ppermute | solution.py:29
  85.2 4.3 %collective-permute-start.7 = (f32[2,8192]{1,0:T(2,128)S(1)}, f32[2,8192]{1,0:T(2,128)S(1)}, u32[]{:S(2)}, u32[]{:S(2)}) collective-permute-start(f32[2,8192]{1,0:T(2,128)S(1)} %pad_maximum_fusion.3), channel_id=1, source_target_pairs={{0,4},{4,0},{8,12},{12,8},{16,20},{20,16},{24,28},{28,24},{1,5},{5... | collective-permute-start | bytes 196616 | tf_op jit(solution)/shard_map/ppermute | solution.py:29
  90.5 4.3 %collective-permute-start.8 = (f32[2,8192]{1,0:T(2,128)S(1)}, f32[2,8192]{1,0:T(2,128)S(1)}, u32[]{:S(2)}, u32[]{:S(2)}) collective-permute-start(f32[2,8192]{1,0:T(2,128)S(1)} %pad_maximum_fusion.4), channel_id=1, source_target_pairs={{0,8},{4,12},{8,0},{12,4},{16,24},{20,28},{24,16},{28,20},{1,9},{5... | collective-permute-start | bytes 196616 | tf_op jit(solution)/shard_map/ppermute | solution.py:29
  95.0 6.7 %collective-permute-start.9 = (f32[2,8192]{1,0:T(2,128)S(1)}, f32[2,8192]{1,0:T(2,128)S(1)}, u32[]{:S(2)}, u32[]{:S(2)}) collective-permute-start(f32[2,8192]{1,0:T(2,128)S(1)} %pad_maximum_fusion.5), channel_id=1, source_target_pairs={{0,16},{4,20},{8,24},{12,28},{16,0},{20,4},{24,8},{28,12},{1,17},{... | collective-permute-start | bytes 196616 | tf_op jit(solution)/shard_map/ppermute | solution.py:29
  123.3 2.0 %collective-permute-start.11 = (f32[2,512,128]{2,1,0:T(8,128)S(1)}, f32[2,512,128]{2,1,0:T(8,128)S(1)}, u32[]{:S(2)}, u32[]{:S(2)}) collective-permute-start(f32[2,512,128]{2,1,0:T(8,128)S(1)} %dynamic-slice_bitcast_fusion), channel_id=1, source_target_pairs={{0,1},{1,0},{2,3},{3,2},{4,5},{5,4},{6,7},{7,6},{8,9},{9,8},{10,11... | collective-permute-start | bytes 1572872 | tf_op jit(solution)/shard_map/ppermute | solution.py:59
  123.4 1.9 %collective-permute-start.10 = (f32[2,2,512]{2,1,0:T(2,128)S(1)}, f32[2,2,512]{2,1,0:T(2,128)S(1)}, u32[]{:S(2)}, u32[]{:S(2)}) collective-permute-start(f32[2,2,512]{2,1,0:T(2,128)S(1)} %pad_maximum_fusion.10), channel_id=1, source_target_pairs={{0,1},{1,0},{2,3},{3,2},{4,5},{5,4},{6,7},{7,6},{8,9},{9,8},{10,11... | collective-permute-start | bytes 24584 | tf_op jit(solution)/shard_map/ppermute | solution.py:58
  126.8 8.5 %collective-permute-start.13 = (f32[1,512,128]{2,1,0:T(8,128)S(1)}, f32[1,512,128]{2,1,0:T(8,128)S(1)}, u32[]{:S(2)}, u32[]{:S(2)}) collective-permute-start(f32[1,512,128]{2,1,0:T(8,128)S(1)} %constant_dynamic-slice_fusion.1), channel_id=1, source_target_pairs={{0,2},{1,3},{2,0},{3,1},{4,6},{5,7},{6,4},{7,5},{8,10},{9,11},{10,... | collective-permute-start | bytes 786440 | tf_op jit(solution)/shard_map/ppermute | solution.py:59
  126.8 8.4 %collective-permute-start.12 = (f32[2,1,512]{2,1,0:T(1,128)S(1)}, f32[2,1,512]{2,1,0:T(1,128)S(1)}, u32[]{:S(2)}, u32[]{:S(2)}) collective-permute-start(f32[2,1,512]{2,1,0:T(1,128)S(1)} %pad_maximum_fusion.11), channel_id=1, source_target_pairs={{0,2},{1,3},{2,0},{3,1},{4,6},{5,7},{6,4},{7,5},{8,10},{9,11},{10,... | collective-permute-start | bytes 12296 | tf_op jit(solution)/shard_map/ppermute | solution.py:58
where the time goes:
time: 138 us; the launch traced here: 136 us
  Pallas kernels  57.9 us (42%)
  waiting for transfers between devices  36.2 us (26%)
  other arithmetic  19.8 us (14%)
  starting transfers between devices  15.7 us (11%)
  local copies, waits for them, and re-layouts  5.75 us (4%)
    ppermute x10, waiting for transfers between devices, butterfly_lse(): other = lax.ppermute(jnp.stack([highest, totals]), axis, pairs)  28.4 us
    pallas_call x2, Pallas kernels, row_pass(): pl.pallas_call(row_kernel, grid_spec=spec, out_shape=[jax.ShapeDtypeStruc...  22.2 us
    pallas_call x2, Pallas kernels, column_pass(): pl.pallas_call(column_kernel, grid_spec=spec, out_shape=[jax.ShapeDtypeSt...  20 us
    pallas_call x1, Pallas kernels, project_pass(): pl.pallas_call(project_kernel, grid_spec=spec, out_shape=[jax.ShapeDtypeS...  15.7 us
    ppermute x10, starting transfers between devices, butterfly_lse(): other = lax.ppermute(jnp.stack([highest, totals]), axis, pairs)  13.1 us
    ppermute x2, waiting for transfers between devices, halving_merge(): small = lax.ppermute(jnp.stack([top_send, den_send]), axis, pairs)  7.81 us
    another operation x10, other arithmetic, butterfly_lse(): other = lax.ppermute(jnp.stack([highest, totals]), axis, pairs)  3.43 us
    unnamed x8, local copies, waits for them, and re-layouts  3.3 us
  transfers between devices with their start and end apart: 14, of which 12 were waited for; matrix products, arithmetic and copies ran while one was open for 0% of the time, Pallas kernels for 0%

commit v1 on v0

v1 whole, which is shorter than its diff:
```python
import functools

import jax
import jax.numpy as jnp
from jax import lax
from jax.experimental import pallas as pl
from jax.experimental.pallas import tpu as pltpu
from jax.sharding import PartitionSpec as P

BLOCK = 256
ITERS = 2


SENTINEL = -1e30
EPSILON = 0.1
SCALE = 1.0 / EPSILON


def lse_pair(top, total, other_top, other_total):
    overall = jnp.maximum(top, other_top)
    return (overall, total * jnp.exp(top - overall) + other_total * jnp.exp(other_top - overall))


def butterfly_lse(highest, totals, axis):
    size = lax.axis_size(axis)
    step = 1
    while step < size:
        pairs = [(i, i ^ step) for i in range(size)]
        other = lax.ppermute(jnp.stack([highest, totals]), axis, pairs)
        highest, totals = lse_pair(highest, totals, other[0], other[1])
        step *= 2
    return (highest, totals)


def halving_merge(top, numerator, denominator, axis):
    size = lax.axis_size(axis)
    me = lax.axis_index(axis)
    rows = top.shape[0] // size
    top = top.reshape(size, rows)
    denominator = denominator.reshape(size, rows)
    numerator = numerator.reshape(size, rows, numerator.shape[-1])
    step = 1
    while step < size:
        pairs = [(i, i ^ step) for i in range(size)]
        keep = (me // step) % 2
        count = top.shape[0] // 2

        def split(x):
            x = x.reshape((count, 2) + x.shape[1:])
            return (
                lax.dynamic_index_in_dim(x, keep, axis=1, keepdims=False),
                lax.dynamic_index_in_dim(x, 1 - keep, axis=1, keepdims=False),
            )

        top_keep, top_send = split(top)
        den_keep, den_send = split(denominator)
        num_keep, num_send = split(numerator)
        small = lax.ppermute(jnp.stack([top_send, den_send]), axis, pairs)
        num_other = lax.ppermute(num_send, axis, pairs)
        overall = jnp.maximum(top_keep, small[0])
        mine = jnp.exp(top_keep - overall)
        theirs = jnp.exp(small[0] - overall)
        numerator = num_keep * mine[..., None] + num_other * theirs[..., None]
        denominator = den_keep * mine + small[1] * theirs
        top = overall
        step *= 2
    return (numerator.reshape(rows, -1), denominator.reshape(rows))


CHUNK = 64


def tile_slice(ref, b):
    return ref[:, pl.ds(pl.multiple_of(b * BLOCK, BLOCK), BLOCK)]


def row_slice(ref, r):
    return ref[pl.ds(pl.multiple_of(r * BLOCK, BLOCK), BLOCK), :]


def doubled_source(src_ref, r):
    exact = tile_slice(src_ref, r).astype(jnp.float32)
    return (exact * 2.0).astype(jnp.bfloat16), jnp.sum(exact * exact, axis=0, keepdims=True)


def products(doubled, tgt_ref, b):
    return lax.dot_general(doubled, tile_slice(tgt_ref, b), (((0,), (0,)), ((), ())),
                           preferred_element_type=jnp.float32)


def as_row(column, scratch):
    scratch[...] = jnp.broadcast_to(column, scratch.shape)
    return jnp.transpose(scratch[...])[0:1, :]


def as_column(row, scratch):
    scratch[...] = jnp.broadcast_to(row, scratch.shape)
    return jnp.transpose(scratch[...])[:, 0:1]


def by_count(live, slots, body):
    for count in range(1, slots + 1):
        pl.when(live == count)(functools.partial(body, count))


def over_rows(rows, body):
    lax.fori_loop(0, rows, lambda r, c: (body(r), c)[1], 0)


def fill_shifted(blocks_ref, r, count, doubled, tgt_ref, tnorm_ref, tpot_ref, held):
    for k in range(count):
        b = blocks_ref[r, k]
        shift = tile_slice(tpot_ref, b) - tile_slice(tnorm_ref, b)
        held[k] = products(doubled, tgt_ref, b) + shift


def chunk_peak(held, count, rows):
    peak = held[0, rows, :]
    for k in range(1, count):
        peak = jnp.maximum(peak, held[k, rows, :])
    return jnp.max(peak, axis=1, keepdims=True)


def row_kernel(blocks_ref, count_ref, src_ref, tgt_ref, tnorm_ref, tpot_ref,
               high_ref, total_ref, held, high_col, total_col, wide):
    def per_row(r):
        doubled, snorm = doubled_source(src_ref, r)

        def body(count):
            fill_shifted(blocks_ref, r, count, doubled, tgt_ref, tnorm_ref, tpot_ref, held)
            for chunk in range(BLOCK // CHUNK):
                rows = pl.ds(chunk * CHUNK, CHUNK)
                peak = chunk_peak(held, count, rows)
                acc = jnp.exp((held[0, rows, :] - peak) * SCALE)
                for k in range(1, count):
                    acc = acc + jnp.exp((held[k, rows, :] - peak) * SCALE)
                high_col[rows, :] = peak
                total_col[rows, :] = jnp.sum(acc, axis=1, keepdims=True)

        by_count(count_ref[r], held.shape[0], body)
        lanes = pl.ds(pl.multiple_of(r * BLOCK, BLOCK), BLOCK)
        high_ref[:, lanes] = (as_row(high_col[...], wide) - snorm) * SCALE
        total_ref[:, lanes] = as_row(total_col[...], wide)

    over_rows(count_ref.shape[0], per_row)


def column_kernel(blocks_ref, count_ref, src_ref, spot_ref, tgt_ref, tnorm_ref,
                  top_ref, sum_ref, tall):
    top_ref[...] = jnp.full(top_ref.shape, SENTINEL, jnp.float32)
    sum_ref[...] = jnp.zeros(sum_ref.shape, jnp.float32)

    def per_row(r):
        doubled, snorm = doubled_source(src_ref, r)
        shift = as_column(tile_slice(spot_ref, r) - snorm, tall)

        def body(count):
            for k in range(count):
                b = blocks_ref[r, k]
                lanes = pl.ds(pl.multiple_of(b * BLOCK, BLOCK), BLOCK)
                shifted = products(doubled, tgt_ref, b) + shift
                peak = jnp.max(shifted, axis=0, keepdims=True)
                totals = jnp.sum(jnp.exp((shifted - peak) * SCALE), axis=0, keepdims=True)
                highest = (peak - tnorm_ref[:, lanes]) * SCALE
                old_top = top_ref[:, lanes]
                new_top = jnp.maximum(old_top, highest)
                sum_ref[:, lanes] = (sum_ref[:, lanes] * jnp.exp(old_top - new_top)
                                     + totals * jnp.exp(highest - new_top))
                top_ref[:, lanes] = new_top

        by_count(count_ref[r], blocks_ref.shape[1], body)

    over_rows(count_ref.shape[0], per_row)


def project_kernel(blocks_ref, count_ref, src_ref, tgt_ref, tnorm_ref, tpot_ref, feat_ref,
                   top_ref, num_ref, den_ref, held, weights, high_col, den_col, wide):
    def per_row(r):
        doubled, snorm = doubled_source(src_ref, r)

        def body(count):
            fill_shifted(blocks_ref, r, count, doubled, tgt_ref, tnorm_ref, tpot_ref, held)
            for chunk in range(BLOCK // CHUNK):
                rows = pl.ds(chunk * CHUNK, CHUNK)
                peak = chunk_peak(held, count, rows)
                acc = jnp.zeros((CHUNK, BLOCK), jnp.float32)
                for k in range(count):
                    rounded = jnp.exp((held[k, rows, :] - peak) * SCALE).astype(jnp.bfloat16)
                    weights[k, rows, :] = rounded
                    acc = acc + rounded.astype(jnp.float32)
                high_col[rows, :] = peak
                den_col[rows, :] = jnp.sum(acc, axis=1, keepdims=True)
            total = None
            for k in range(count):
                part = lax.dot_general(weights[k], tile_slice(feat_ref, blocks_ref[r, k]),
                                       (((1,), (1,)), ((), ())),
                                       preferred_element_type=jnp.float32)
                total = part if total is None else total + part
            num_ref[pl.ds(pl.multiple_of(r * BLOCK, BLOCK), BLOCK), :] = total

        by_count(count_ref[r], held.shape[0], body)
        lanes = pl.ds(pl.multiple_of(r * BLOCK, BLOCK), BLOCK)
        top_ref[:, lanes] = (as_row(high_col[...], wide) - snorm) * SCALE
        den_ref[:, lanes] = as_row(den_col[...], wide)

    over_rows(count_ref.shape[0], per_row)


def whole(shape):
    return pl.BlockSpec(shape, lambda r, *_: (0,) * len(shape))


def column_scratch():
    return pltpu.VMEM((BLOCK, 1), jnp.float32)


def local_call(kernel, operands, outs, scratch):
    spec = pltpu.PrefetchScalarGridSpec(
        num_scalar_prefetch=2,
        grid=(1,),
        in_specs=[whole(x.shape) for x in operands[2:]],
        out_specs=[whole(o.shape) for o in outs],
        scratch_shapes=scratch,
    )
    return pl.pallas_call(kernel, grid_spec=spec, out_shape=outs)(*operands)


def row_pass(blocks, counts, src, tgt, tnorm, tpot):
    rows = src.shape[1]
    slots = blocks.shape[1]
    return local_call(
        row_kernel, (blocks, counts, src, tgt, tnorm, tpot),
        [jax.ShapeDtypeStruct((1, rows), jnp.float32)] * 2,
        [pltpu.VMEM((slots, BLOCK, BLOCK), jnp.float32), column_scratch(), column_scratch(),
         pltpu.VMEM((BLOCK, 128), jnp.float32)],
    )


def column_pass(blocks, counts, src, spot, tgt, tnorm):
    return local_call(
        column_kernel, (blocks, counts, src, spot, tgt, tnorm),
        [jax.ShapeDtypeStruct(tnorm.shape, jnp.float32)] * 2,
        [pltpu.VMEM((128, BLOCK), jnp.float32)],
    )


def project_pass(blocks, counts, src, tgt, tnorm, tpot, feat):
    rows = src.shape[1]
    slots = blocks.shape[1]
    return local_call(
        project_kernel, (blocks, counts, src, tgt, tnorm, tpot, feat),
        [jax.ShapeDtypeStruct((1, rows), jnp.float32),
         jax.ShapeDtypeStruct((rows, feat.shape[0]), jnp.float32),
         jax.ShapeDtypeStruct((1, rows), jnp.float32)],
        [pltpu.VMEM((slots, BLOCK, BLOCK), jnp.float32),
         pltpu.VMEM((slots, BLOCK, BLOCK), jnp.bfloat16),
         column_scratch(), column_scratch(), pltpu.VMEM((BLOCK, 128), jnp.float32)],
    )


def shards(src_emb, tgt_emb, target_features, src_mass, tgt_mass, kept_blocks, kept_count):
    src_rows = src_emb.shape[1]
    tgt_rows = tgt_emb.shape[1]
    src_t = src_emb
    tnorm = jnp.sum(jnp.square(tgt_emb.astype(jnp.float32)), axis=0).reshape(1, tgt_rows)
    counts = kept_count.reshape(-1)

    tgt_potential = jnp.zeros((tgt_rows,), jnp.float32)
    src_potential = jnp.zeros((src_rows,), jnp.float32)
    for iteration in range(ITERS):
        tpot = tgt_potential.reshape(1, tgt_rows)
        highest, totals = row_pass(kept_blocks, counts, src_t, tgt_emb, tnorm, tpot)
        highest, totals = butterfly_lse(highest.reshape(src_rows), totals.reshape(src_rows), "tgt")
        src_potential = EPSILON * jnp.log(src_mass) - EPSILON * (highest + jnp.log(totals))
        block_top, block_sum = column_pass(
            kept_blocks, counts, src_t, src_potential.reshape(1, src_rows), tgt_emb, tnorm
        )
        block_top, block_sum = butterfly_lse(
            block_top.reshape(tgt_rows), block_sum.reshape(tgt_rows), "src"
        )
        tgt_potential = EPSILON * jnp.log(tgt_mass) - EPSILON * (block_top + jnp.log(block_sum))

    tpot = tgt_potential.reshape(1, tgt_rows)
    local_top, numerator, denominator = project_pass(
        kept_blocks, counts, src_t, tgt_emb, tnorm, tpot, target_features
    )
    numerator, denominator = halving_merge(
        local_top.reshape(src_rows), numerator, denominator.reshape(src_rows), "tgt"
    )
    projected = numerator / denominator[:, None]
    return (projected, src_potential, tgt_potential)


def solution(mesh):
    return jax.shard_map(
        shards,
        mesh=mesh,
        in_specs=(
            P(None, "src"),
            P(None, "tgt"),
            P(None, "tgt"),
            P("src"),
            P("tgt"),
            P("src", "tgt"),
            P("src", "tgt"),
        ),
        out_specs=(P(("src", "tgt"), None), P("src"), P("tgt")),
        check_vma=False,
    )
```

time: 138 us -> 131 us (0.949)
  the two profiles are of different devices: /device:TPU:0 before, /device:TPU:12 now
where the time goes in v1:
time: 131 us; the launch traced here: 129 us
  Pallas kernels  57.1 us (44%)
  waiting for transfers between devices  45.4 us (35%)
  other arithmetic  19.8 us (15%)
  starting transfers between devices  3.35 us (3%)
  local copies, waits for them, and re-layouts  2.47 us (2%)
    pallas_call x5, Pallas kernels, local_call(): return pl.pallas_call(kernel, grid_spec=spec, out_shape=outs)(*operands)  57.1 us
    ppermute x10, waiting for transfers between devices, butterfly_lse(): other = lax.ppermute(jnp.stack([highest, totals]), axis, pairs)  37.6 us
    ppermute x2, waiting for transfers between devices, halving_merge(): small = lax.ppermute(jnp.stack([top_send, den_send]), axis, pairs)  7.81 us
    another operation x10, other arithmetic, butterfly_lse(): other = lax.ppermute(jnp.stack([highest, totals]), axis, pairs)  3.43 us
    sub x2, other arithmetic, shards(): EPSILON * jnp.log(tgt_mass) - EPSILON * (block_top + jnp.log(block_sum))  2.91 us
    pallas_call x2, other arithmetic, local_call(): return pl.pallas_call(kernel, grid_spec=spec, out_shape=outs)(*operands)  2.73 us
    sub x2, other arithmetic, shards(): EPSILON * jnp.log(src_mass) - EPSILON * (highest + jnp.log(totals))  2.69 us
  transfers between devices with their start and end apart: 14, of which 12 were waited for; matrix products, arithmetic and copies ran while one was open for 0% of the time, Pallas kernels for 0%

profile of v1, /device:TPU:12, one launch (start us, length us, event | category | flops | bytes accessed | tf_op | source)
XLA Modules:
  0.0 129.1 jit_solution(12043851241229830706)
XLA Ops:
  0.6 2.1 %multiply_reduce_fusion = f32[8192]{0:T(1024)} fusion(bf16[64,8192]{1,0:T(8,128)(2,1)} %tgt_ref.9), kind=kLoop, calls=%fused_computation | loop fusion | flops 1564672 | bytes 1081344 | tf_op jit(solution)/shard_map/reduce_sum | solution.py:265
  3.4 10.7 %shard_map.94 = (f32[1,2048]{1,0:T(1,128)}, f32[1,2048]{1,0:T(1,128)}) custom-call(s32[8,8]{1,0:T(8,128)} %blocks_ref.9, s32[8]{0:T(128)} %bitcast.136, bf16[64,2048]{1,0:T(8,128)(2,1)} %src_ref.9, bf16[64,8192]{1,0:T(8,128)(2,1)} %tgt_ref.9, f32[1,8192]{1,0:T(1,128)} %bitcast.95, f32[1,8192]{1,0:T(1,128)} %reshape.111.tpot_ref), custom_call_target="tpu_custom_call" | custom-call | tf_op jit(solution)/shard_map/pallas_call | solution.py:225
  16.9 3.7 %collective-permute-done.1 = f32[2,2048]{1,0:T(2,128)S(1)} collective-permute-done((f32[2,2048]{1,0:T(2,128)S(1)}, f32[2,2048]{1,0:T(2,128)S(1)}, u32[]{:S(2)}, u32[]{:S(2)}) %collective-permute-start.1) | collective-permute-done | bytes 16416 | tf_op jit(solution)/shard_map/ppermute | solution.py:29
  20.7 1.3 %multiply_subtract_fusion.3 = f32[2048]{0:T(1024)} fusion(f32[2048]{0:T(1024)S(1)} %bitcast.127, f32[2048]{0:T(1024)S(1)} %bitcast.126, f32[2048]{0:T(1024)S(1)} %bitcast.131, f32[2048]{0:T(1024)S(1)} %bitcast.130, f32[2048]{0:T(1024)} %bitcast.120, f32[2048]{0:T(1024)} %bitcast.121, f32[2048]{0:T(1024)S(1)} %copy-done.1), kind=kLoop, calls=%fused_computation.49 | loop fusion | flops 32768 | bytes 65536 | tf_op jit(solution)/shard_map/sub | solution.py:274
  22.0 9.7 %shard_map.95 = (f32[1,8192]{1,0:T(1,128)}, f32[1,8192]{1,0:T(1,128)}) custom-call(s32[8,8]{1,0:T(8,128)} %blocks_ref.9, s32[8]{0:T(128)} %bitcast.137, bf16[64,2048]{1,0:T(8,128)(2,1)} %src_ref.9, f32[1,2048]{1,0:T(1,128)} %bitcast.125, bf16[64,8192]{1,0:T(8,128)(2,1)} %tgt_ref.9, f32[1,8192]{1,0:T(1,128)} %bitcast.96), custom_call_target="tpu_custom_call" | custom-call | tf_op jit(solution)/shard_map/pallas_call | solution.py:225
  32.7 4.3 %collective-permute-done.2 = f32[2,8192]{1,0:T(2,128)S(1)} collective-permute-done((f32[2,8192]{1,0:T(2,128)S(1)}, f32[2,8192]{1,0:T(2,128)S(1)}, u32[]{:S(2)}, u32[]{:S(2)}) %collective-permute-start.2) | collective-permute-done | bytes 65568 | tf_op jit(solution)/shard_map/ppermute | solution.py:29
  38.0 4.8 %collective-permute-done.3 = f32[2,8192]{1,0:T(2,128)S(1)} collective-permute-done((f32[2,8192]{1,0:T(2,128)S(1)}, f32[2,8192]{1,0:T(2,128)S(1)}, u32[]{:S(2)}, u32[]{:S(2)}) %collective-permute-start.3) | collective-permute-done | bytes 65568 | tf_op jit(solution)/shard_map/ppermute | solution.py:29
  43.0 5.2 %collective-permute-done.4 = f32[2,8192]{1,0:T(2,128)S(1)} collective-permute-done((f32[2,8192]{1,0:T(2,128)S(1)}, f32[2,8192]{1,0:T(2,128)S(1)}, u32[]{:S(2)}, u32[]{:S(2)}) %collective-permute-start.4) | collective-permute-done | bytes 65568 | tf_op jit(solution)/shard_map/ppermute | solution.py:29
  48.2 1.5 %multiply_subtract_fusion.1 = f32[8192]{0:T(1024)} fusion(f32[8192]{0:T(1024)S(1)} %bitcast.109, f32[8192]{0:T(1024)S(1)} %bitcast.108, f32[8192]{0:T(1024)S(1)} %bitcast.119, f32[8192]{0:T(1024)S(1)} %bitcast.118, f32[8192]{0:T(1024)S(1)} %bitcast.117, f32[8192]{0:T(1024)S(1)} %bitcast.116, f32[8192]{0:T(1024)} %bitcast.104, f32[8192]{0:T(1024)} %bitcast.105, ...), kind=kLoop, calls=%fused_computation.23 | loop fusion | flops 180224 | bytes 327680 | tf_op jit(solution)/shard_map/sub | solution.py:281
  49.7 10.7 %shard_map.96 = (f32[1,2048]{1,0:T(1,128)}, f32[1,2048]{1,0:T(1,128)}) custom-call(s32[8,8]{1,0:T(8,128)} %blocks_ref.9, s32[8]{0:T(128)} %bitcast.138, bf16[64,2048]{1,0:T(8,128)(2,1)} %src_ref.9, bf16[64,8192]{1,0:T(8,128)(2,1)} %tgt_ref.9, f32[1,8192]{1,0:T(1,128)} %bitcast.97, f32[1,8192]{1,0:T(1,128)} %bitcast.107), custom_call_target="tpu_custom_call" | custom-call | tf_op jit(solution)/shard_map/pallas_call | solution.py:225
  63.2 3.7 %collective-permute-done.6 = f32[2,2048]{1,0:T(2,128)S(1)} collective-permute-done((f32[2,2048]{1,0:T(2,128)S(1)}, f32[2,2048]{1,0:T(2,128)S(1)}, u32[]{:S(2)}, u32[]{:S(2)}) %collective-permute-start.6) | collective-permute-done | bytes 16416 | tf_op jit(solution)/shard_map/ppermute | solution.py:29
  67.0 1.3 %multiply_subtract_fusion.2 = f32[2048]{0:T(1024)} fusion(f32[2048]{0:T(1024)S(1)} %bitcast.129, f32[2048]{0:T(1024)S(1)} %bitcast.128, f32[2048]{0:T(1024)S(1)} %bitcast.133, f32[2048]{0:T(1024)S(1)} %bitcast.132, f32[2048]{0:T(1024)} %bitcast.122, f32[2048]{0:T(1024)} %bitcast.123, f32[2048]{0:T(1024)S(1)} %copy-done.1), kind=kLoop, calls=%fused_computation.41 | loop fusion | flops 32768 | bytes 65536 | tf_op jit(solution)/shard_map/sub | solution.py:274
  68.3 9.7 %shard_map.97 = (f32[1,8192]{1,0:T(1,128)}, f32[1,8192]{1,0:T(1,128)}) custom-call(s32[8,8]{1,0:T(8,128)} %blocks_ref.9, s32[8]{0:T(128)} %bitcast.139, bf16[64,2048]{1,0:T(8,128)(2,1)} %src_ref.9, f32[1,2048]{1,0:T(1,128)} %bitcast.124, bf16[64,8192]{1,0:T(8,128)(2,1)} %tgt_ref.9, f32[1,8192]{1,0:T(1,128)} %bitcast.98), custom_call_target="tpu_custom_call" | custom-call | tf_op jit(solution)/shard_map/pallas_call | solution.py:225
  79.0 4.3 %collective-permute-done.7 = f32[2,8192]{1,0:T(2,128)S(1)} collective-permute-done((f32[2,8192]{1,0:T(2,128)S(1)}, f32[2,8192]{1,0:T(2,128)S(1)}, u32[]{:S(2)}, u32[]{:S(2)}) %collective-permute-start.7) | collective-permute-done | bytes 65568 | tf_op jit(solution)/shard_map/ppermute | solution.py:29
  84.3 4.3 %collective-permute-done.8 = f32[2,8192]{1,0:T(2,128)S(1)} collective-permute-done((f32[2,8192]{1,0:T(2,128)S(1)}, f32[2,8192]{1,0:T(2,128)S(1)}, u32[]{:S(2)}, u32[]{:S(2)}) %collective-permute-start.8) | collective-permute-done | bytes 65568 | tf_op jit(solution)/shard_map/ppermute | solution.py:29
  88.8 5.1 %collective-permute-done.9 = f32[2,8192]{1,0:T(2,128)S(1)} collective-permute-done((f32[2,8192]{1,0:T(2,128)S(1)}, f32[2,8192]{1,0:T(2,128)S(1)}, u32[]{:S(2)}, u32[]{:S(2)}) %collective-permute-start.9) | collective-permute-done | bytes 65568 | tf_op jit(solution)/shard_map/ppermute | solution.py:29
  94.0 1.5 %multiply_subtract_fusion = f32[8192]{0:T(1024)} fusion(f32[8192]{0:T(1024)S(1)} %bitcast.111, f32[8192]{0:T(1024)S(1)} %bitcast.110, f32[8192]{0:T(1024)S(1)} %bitcast.115, f32[8192]{0:T(1024)S(1)} %bitcast.114, f32[8192]{0:T(1024)S(1)} %bitcast.113, f32[8192]{0:T(1024)S(1)} %bitcast.112, f32[8192]{0:T(1024)} %bitcast.102, f32[8192]{0:T(1024)} %bitcast.103, ...), kind=kLoop, calls=%fused_computation.11 | loop fusion | flops 180224 | bytes 327680 | tf_op jit(solution)/shard_map/sub | solution.py:281
  95.5 16.2 %shard_map.98 = (f32[1,2048]{1,0:T(1,128)}, f32[2048,128]{1,0:T(8,128)}, f32[1,2048]{1,0:T(1,128)}) custom-call(s32[8,8]{1,0:T(8,128)} %blocks_ref.9, s32[8]{0:T(128)} %bitcast.140, bf16[64,2048]{1,0:T(8,128)(2,1)} %src_ref.9, bf16[64,8192]{1,0:T(8,128)(2,1)} %tgt_ref.9, f32[1,8192]{1,0:T(1,128)} %bitcast.99, f32[1,8192]{1,0:T(1,128)} %bitcast.106, ...), custom_call_target="tpu_custom_call" | custom-call | tf_op jit(solution)/shard_map/pallas_call | solution.py:225
  112.2 1.4 %reduce.7 = f32[2048]{0:T(1024)S(1)} reduce(f32[1,2048]{1,0:T(1,128)} %get-tuple-element.23, f32[]{:T(128)} %broadcast.29), dimensions={0}, to_apply=%get-tuple-element.23.reduce_sub_computation.3 | reduce | bytes 16388 | tf_op jit(solution)/shard_map/pallas_call | solution.py:225
  113.6 1.4 %reduce.6 = f32[2048]{0:T(1024)S(1)} reduce(f32[1,2048]{1,0:T(1,128)} %get-tuple-element.24, f32[]{:T(128)} %broadcast.29), dimensions={0}, to_apply=%get-tuple-element.24.reduce_sub_computation.3 | reduce | bytes 16388 | tf_op jit(solution)/shard_map/pallas_call | solution.py:225
  116.7 1.4 %collective-permute-done.10 = f32[2,2,512]{2,1,0:T(2,128)S(1)} collective-permute-done((f32[2,2,512]{2,1,0:T(2,128)S(1)}, f32[2,2,512]{2,1,0:T(2,128)S(1)}, u32[]{:S(2)}, u32[]{:S(2)}) %collective-permute-start.10) | collective-permute-done | bytes 8224 | tf_op jit(solution)/shard_map/ppermute | solution.py:58
  118.2 1.4 %fusion = f32[2,512,128]{2,1,0:T(8,128)S(1)} fusion(f32[2,512,128]{2,1,0:T(8,128)S(1)} %collective-permute-done.11, f32[2,2,512,128]{3,2,1,0:T(8,128)} %bitcast.101, s32[]{:T(128)S(6)} %select_n.41, f32[2,512]{1,0:T(2,128)S(1)} %get-tuple-element.30, f32[2,512]{1,0:T(2,128)S(1)} %get-tuple-element.29), kind=kLoop, calls=%fused_computation.2 | loop fusion | flops 393216 | bytes 1581060 | tf_op jit(solution)/shard_map/add | solution.py:63
  119.7 2.0 %collective-permute-start.12 = (f32[2,1,512]{2,1,0:T(1,128)S(1)}, f32[2,1,512]{2,1,0:T(1,128)S(1)}, u32[]{:S(2)}, u32[]{:S(2)}) collective-permute-start(f32[2,1,512]{2,1,0:T(1,128)S(1)} %pad_maximum_fusion.11), channel_id=1, source_target_pairs={{0,2},{1,3},{2,0},{3,1},{4,6},{5,7},{6,4},{7,5},{8,10},{9,11},{10,... | collective-permute-start | bytes 12296 | tf_op jit(solution)/shard_map/ppermute | solution.py:58
  121.7 6.4 %collective-permute-done.12 = f32[2,1,512]{2,1,0:T(1,128)S(1)} collective-permute-done((f32[2,1,512]{2,1,0:T(1,128)S(1)}, f32[2,1,512]{2,1,0:T(1,128)S(1)}, u32[]{:S(2)}, u32[]{:S(2)}) %collective-permute-start.12) | collective-permute-done | bytes 4128 | tf_op jit(solution)/shard_map/ppermute | solution.py:58
  (57 shorter events, 14.2 us)
Async XLA Ops:
  0.6 20.0 %copy-start.1 = (f32[2048]{0:T(1024)S(1)}, f32[2048]{0:T(1024)}, u32[]{:S(2)}) copy-start(f32[2048]{0:T(1024)} %param.10) | copy-start | bytes 24580
  2.7 45.5 %copy-start = (f32[8192]{0:T(1024)S(1)}, f32[8192]{0:T(1024)}, u32[]{:S(2)}) copy-start(f32[8192]{0:T(1024)} %param.11) | copy-start | bytes 98308
  14.8 1.2 collective-permute-start
  16.8 3.8 %collective-permute-start.1 = (f32[2,2048]{1,0:T(2,128)S(1)}, f32[2,2048]{1,0:T(2,128)S(1)}, u32[]{:S(2)}, u32[]{:S(2)}) collective-permute-start(f32[2,2048]{1,0:T(2,128)S(1)} %pad_maximum_fusion.7), channel_id=1, source_target_pairs={{0,2},{1,3},{2,0},{3,1},{4,6},{5,7},{6,4},{7,5},{8,10},{9,11},{10,... | collective-permute-start | bytes 49160 | tf_op jit(solution)/shard_map/ppermute | solution.py:29
  32.6 4.3 %collective-permute-start.2 = (f32[2,8192]{1,0:T(2,128)S(1)}, f32[2,8192]{1,0:T(2,128)S(1)}, u32[]{:S(2)}, u32[]{:S(2)}) collective-permute-start(f32[2,8192]{1,0:T(2,128)S(1)} %pad_maximum_fusion), channel_id=1, source_target_pairs={{0,4},{4,0},{8,12},{12,8},{16,20},{20,16},{24,28},{28,24},{1,5},{5... | collective-permute-start | bytes 196616 | tf_op jit(solution)/shard_map/ppermute | solution.py:29
  37.9 4.8 %collective-permute-start.3 = (f32[2,8192]{1,0:T(2,128)S(1)}, f32[2,8192]{1,0:T(2,128)S(1)}, u32[]{:S(2)}, u32[]{:S(2)}) collective-permute-start(f32[2,8192]{1,0:T(2,128)S(1)} %pad_maximum_fusion.1), channel_id=1, source_target_pairs={{0,8},{4,12},{8,0},{12,4},{16,24},{20,28},{24,16},{28,20},{1,9},{5... | collective-permute-start | bytes 196616 | tf_op jit(solution)/shard_map/ppermute | solution.py:29
  42.9 5.2 %collective-permute-start.4 = (f32[2,8192]{1,0:T(2,128)S(1)}, f32[2,8192]{1,0:T(2,128)S(1)}, u32[]{:S(2)}, u32[]{:S(2)}) collective-permute-start(f32[2,8192]{1,0:T(2,128)S(1)} %pad_maximum_fusion.2), channel_id=1, source_target_pairs={{0,16},{4,20},{8,24},{12,28},{16,0},{20,4},{24,8},{28,12},{1,17},{... | collective-permute-start | bytes 196616 | tf_op jit(solution)/shard_map/ppermute | solution.py:29
  61.1 1.2 collective-permute-start.5
  63.2 3.8 %collective-permute-start.6 = (f32[2,2048]{1,0:T(2,128)S(1)}, f32[2,2048]{1,0:T(2,128)S(1)}, u32[]{:S(2)}, u32[]{:S(2)}) collective-permute-start(f32[2,2048]{1,0:T(2,128)S(1)} %pad_maximum_fusion.9), channel_id=1, source_target_pairs={{0,2},{1,3},{2,0},{3,1},{4,6},{5,7},{6,4},{7,5},{8,10},{9,11},{10,... | collective-permute-start | bytes 49160 | tf_op jit(solution)/shard_map/ppermute | solution.py:29
  78.9 4.3 %collective-permute-start.7 = (f32[2,8192]{1,0:T(2,128)S(1)}, f32[2,8192]{1,0:T(2,128)S(1)}, u32[]{:S(2)}, u32[]{:S(2)}) collective-permute-start(f32[2,8192]{1,0:T(2,128)S(1)} %pad_maximum_fusion.3), channel_id=1, source_target_pairs={{0,4},{4,0},{8,12},{12,8},{16,20},{20,16},{24,28},{28,24},{1,5},{5... | collective-permute-start | bytes 196616 | tf_op jit(solution)/shard_map/ppermute | solution.py:29
  84.2 4.3 %collective-permute-start.8 = (f32[2,8192]{1,0:T(2,128)S(1)}, f32[2,8192]{1,0:T(2,128)S(1)}, u32[]{:S(2)}, u32[]{:S(2)}) collective-permute-start(f32[2,8192]{1,0:T(2,128)S(1)} %pad_maximum_fusion.4), channel_id=1, source_target_pairs={{0,8},{4,12},{8,0},{12,4},{16,24},{20,28},{24,16},{28,20},{1,9},{5... | collective-permute-start | bytes 196616 | tf_op jit(solution)/shard_map/ppermute | solution.py:29
  88.7 5.2 %collective-permute-start.9 = (f32[2,8192]{1,0:T(2,128)S(1)}, f32[2,8192]{1,0:T(2,128)S(1)}, u32[]{:S(2)}, u32[]{:S(2)}) collective-permute-start(f32[2,8192]{1,0:T(2,128)S(1)} %pad_maximum_fusion.5), channel_id=1, source_target_pairs={{0,16},{4,20},{8,24},{12,28},{16,0},{20,4},{24,8},{28,12},{1,17},{... | collective-permute-start | bytes 196616 | tf_op jit(solution)/shard_map/ppermute | solution.py:29
  116.1 2.0 %collective-permute-start.11 = (f32[2,512,128]{2,1,0:T(8,128)S(1)}, f32[2,512,128]{2,1,0:T(8,128)S(1)}, u32[]{:S(2)}, u32[]{:S(2)}) collective-permute-start(f32[2,512,128]{2,1,0:T(8,128)S(1)} %dynamic-slice_bitcast_fusion), channel_id=1, source_target_pairs={{0,1},{1,0},{2,3},{3,2},{4,5},{5,4},{6,7},{7,6},{8,9},{9,8},{10,11... | collective-permute-start | bytes 1572872 | tf_op jit(solution)/shard_map/ppermute | solution.py:59
  116.2 1.9 %collective-permute-start.10 = (f32[2,2,512]{2,1,0:T(2,128)S(1)}, f32[2,2,512]{2,1,0:T(2,128)S(1)}, u32[]{:S(2)}, u32[]{:S(2)}) collective-permute-start(f32[2,2,512]{2,1,0:T(2,128)S(1)} %pad_maximum_fusion.10), channel_id=1, source_target_pairs={{0,1},{1,0},{2,3},{3,2},{4,5},{5,4},{6,7},{7,6},{8,9},{9,8},{10,11... | collective-permute-start | bytes 24584 | tf_op jit(solution)/shard_map/ppermute | solution.py:58
  119.6 8.5 %collective-permute-start.13 = (f32[1,512,128]{2,1,0:T(8,128)S(1)}, f32[1,512,128]{2,1,0:T(8,128)S(1)}, u32[]{:S(2)}, u32[]{:S(2)}) collective-permute-start(f32[1,512,128]{2,1,0:T(8,128)S(1)} %constant_dynamic-slice_fusion.1), channel_id=1, source_target_pairs={{0,2},{1,3},{2,0},{3,1},{4,6},{5,7},{6,4},{7,5},{8,10},{9,11},{10,... | collective-permute-start | bytes 786440 | tf_op jit(solution)/shard_map/ppermute | solution.py:59
  119.7 8.4 %collective-permute-start.12 = (f32[2,1,512]{2,1,0:T(1,128)S(1)}, f32[2,1,512]{2,1,0:T(1,128)S(1)}, u32[]{:S(2)}, u32[]{:S(2)}) collective-permute-start(f32[2,1,512]{2,1,0:T(1,128)S(1)} %pad_maximum_fusion.11), channel_id=1, source_target_pairs={{0,2},{1,3},{2,0},{3,1},{4,6},{5,7},{6,4},{7,5},{8,10},{9,11},{10,... | collective-permute-start | bytes 12296 | tf_op jit(solution)/shard_map/ppermute | solution.py:58

commit v2 on v1

--- a/solution.py
+++ b/solution.py
@@ -1,4 +1,5 @@
 import functools
+import math
 
 import jax
 import jax.numpy as jnp
@@ -14,6 +15,7 @@
 SENTINEL = -1e30
 EPSILON = 0.1
 SCALE = 1.0 / EPSILON
+BASE2 = SCALE / math.log(2.0)
 
 
 def lse_pair(top, total, other_top, other_total):
@@ -68,6 +70,7 @@
 
 
 CHUNK = 64
+EXTRA = 16
 
 
 def tile_slice(ref, b):
@@ -131,9 +134,9 @@
             for chunk in range(BLOCK // CHUNK):
                 rows = pl.ds(chunk * CHUNK, CHUNK)
                 peak = chunk_peak(held, count, rows)
-                acc = jnp.exp((held[0, rows, :] - peak) * SCALE)
+                acc = jnp.exp2((held[0, rows, :] - peak) * BASE2)
                 for k in range(1, count):
-                    acc = acc + jnp.exp((held[k, rows, :] - peak) * SCALE)
+                    acc = acc + jnp.exp2((held[k, rows, :] - peak) * BASE2)
                 high_col[rows, :] = peak
                 total_col[rows, :] = jnp.sum(acc, axis=1, keepdims=True)
 
@@ -145,22 +148,38 @@
     over_rows(count_ref.shape[0], per_row)
 
 
+def split_rows(row, ones):
+    high = row.astype(jnp.bfloat16).astype(jnp.float32)
+    middle = (row - high).astype(jnp.bfloat16).astype(jnp.float32)
+    low = row - high - middle
+    index = lax.broadcasted_iota(jnp.int32, (EXTRA, row.shape[1]), 0)
+    if ones:
+        rows = jnp.where(index < 3, 1.0, 0.0)
+    else:
+        rows = jnp.where(index == 0, high, jnp.where(index == 1, middle,
+                                                     jnp.where(index == 2, low, 0.0)))
+    return rows.astype(jnp.bfloat16)
+
+
 def column_kernel(blocks_ref, count_ref, src_ref, spot_ref, tgt_ref, tnorm_ref,
-                  top_ref, sum_ref, tall):
+                  top_ref, sum_ref, lhs):
     top_ref[...] = jnp.full(top_ref.shape, SENTINEL, jnp.float32)
     sum_ref[...] = jnp.zeros(sum_ref.shape, jnp.float32)
+    width = src_ref.shape[0]
 
     def per_row(r):
         doubled, snorm = doubled_source(src_ref, r)
-        shift = as_column(tile_slice(spot_ref, r) - snorm, tall)
+        lhs[0:width, :] = doubled
+        lhs[width:, :] = split_rows(tile_slice(spot_ref, r) - snorm, False)
+        augmented = lhs[...]
 
         def body(count):
             for k in range(count):
                 b = blocks_ref[r, k]
                 lanes = pl.ds(pl.multiple_of(b * BLOCK, BLOCK), BLOCK)
-                shifted = products(doubled, tgt_ref, b) + shift
+                shifted = products(augmented, tgt_ref, b)
                 peak = jnp.max(shifted, axis=0, keepdims=True)
-                totals = jnp.sum(jnp.exp((shifted - peak) * SCALE), axis=0, keepdims=True)
+                totals = jnp.sum(jnp.exp2((shifted - peak) * BASE2), axis=0, keepdims=True)
                 highest = (peak - tnorm_ref[:, lanes]) * SCALE
                 old_top = top_ref[:, lanes]
                 new_top = jnp.maximum(old_top, highest)
@@ -185,7 +204,7 @@
                 peak = chunk_peak(held, count, rows)
                 acc = jnp.zeros((CHUNK, BLOCK), jnp.float32)
                 for k in range(count):
-                    rounded = jnp.exp((held[k, rows, :] - peak) * SCALE).astype(jnp.bfloat16)
+                    rounded = jnp.exp2((held[k, rows, :] - peak) * BASE2).astype(jnp.bfloat16)
                     weights[k, rows, :] = rounded
                     acc = acc + rounded.astype(jnp.float32)
                 high_col[rows, :] = peak
@@ -236,11 +255,11 @@
     )
 
 
-def column_pass(blocks, counts, src, spot, tgt, tnorm):
+def column_pass(blocks, counts, src, spot, tgt_ones, tnorm):
     return local_call(
-        column_kernel, (blocks, counts, src, spot, tgt, tnorm),
+        column_kernel, (blocks, counts, src, spot, tgt_ones, tnorm),
         [jax.ShapeDtypeStruct(tnorm.shape, jnp.float32)] * 2,
-        [pltpu.VMEM((128, BLOCK), jnp.float32)],
+        [pltpu.VMEM((src.shape[0] + EXTRA, BLOCK), jnp.bfloat16)],
     )
 
 
@@ -264,6 +283,9 @@
     src_t = src_emb
     tnorm = jnp.sum(jnp.square(tgt_emb.astype(jnp.float32)), axis=0).reshape(1, tgt_rows)
     counts = kept_count.reshape(-1)
+    tgt_ones = jnp.concatenate(
+        [tgt_emb, split_rows(jnp.zeros((1, tgt_rows), jnp.float32), True)], axis=0
+    )
 
     tgt_potential = jnp.zeros((tgt_rows,), jnp.float32)
     src_potential = jnp.zeros((src_rows,), jnp.float32)
@@ -273,7 +295,7 @@
         highest, totals = butterfly_lse(highest.reshape(src_rows), totals.reshape(src_rows), "tgt")
         src_potential = EPSILON * jnp.log(src_mass) - EPSILON * (highest + jnp.log(totals))
         block_top, block_sum = column_pass(
-            kept_blocks, counts, src_t, src_potential.reshape(1, src_rows), tgt_emb, tnorm
+            kept_blocks, counts, src_t, src_potential.reshape(1, src_rows), tgt_ones, tnorm
         )
         block_top, block_sum = butterfly_lse(
             block_top.reshape(tgt_rows), block_sum.reshape(tgt_rows), "src"

time: 131 us -> 123 us (0.939)
  the two profiles are of different devices: /device:TPU:12 before, /device:TPU:0 now
where the time goes in v2:
time: 123 us; the launch traced here: 121 us
  Pallas kernels  41.7 us (34%)
  starting transfers between devices  27.5 us (22%)
  waiting for transfers between devices  27.5 us (22%)
  other arithmetic  20.6 us (17%)
  local copies, waits for them, and re-layouts  2.56 us (2%)
    pallas_call x5, Pallas kernels, local_call(): return pl.pallas_call(kernel, grid_spec=spec, out_shape=outs)(*operands)  41.7 us
    ppermute x10, starting transfers between devices, butterfly_lse(): other = lax.ppermute(jnp.stack([highest, totals]), axis, pairs)  21.8 us
    ppermute x10, waiting for transfers between devices, butterfly_lse(): other = lax.ppermute(jnp.stack([highest, totals]), axis, pairs)  19.5 us
    ppermute x2, waiting for transfers between devices, halving_merge(): small = lax.ppermute(jnp.stack([top_send, den_send]), axis, pairs)  8.06 us
    ppermute x2, starting transfers between devices, halving_merge(): num_other = lax.ppermute(num_send, axis, pairs)  5.48 us
    another operation x10, other arithmetic, butterfly_lse(): other = lax.ppermute(jnp.stack([highest, totals]), axis, pairs)  3.48 us
    sub x2, other arithmetic, shards(): EPSILON * jnp.log(tgt_mass) - EPSILON * (block_top + jnp.log(block_sum))  2.91 us
    pallas_call x2, other arithmetic, local_call(): return pl.pallas_call(kernel, grid_spec=spec, out_shape=outs)(*operands)  2.73 us
  transfers between devices with their start and end apart: 14, of which 12 were waited for; matrix products, arithmetic and copies ran while one was open for 1% of the time, Pallas kernels for 0%

profile of v2, /device:TPU:0, one launch (start us, length us, event | category | flops | bytes accessed | tf_op | source)
XLA Modules:
  0.0 120.8 jit_solution(13466812113879132682)
XLA Ops:
  0.6 2.2 %multiply_reduce_fusion = f32[8192]{0:T(1024)} fusion(bf16[64,8192]{1,0:T(8,128)(2,1)} %tgt_ref.5), kind=kLoop, calls=%fused_computation | loop fusion | flops 1564672 | bytes 1081344 | tf_op jit(solution)/shard_map/reduce_sum | solution.py:284
  3.5 8.4 %shard_map.94 = (f32[1,2048]{1,0:T(1,128)}, f32[1,2048]{1,0:T(1,128)}) custom-call(s32[8,8]{1,0:T(8,128)} %blocks_ref.9, s32[8]{0:T(128)} %bitcast.136, bf16[64,2048]{1,0:T(8,128)(2,1)} %src_ref.9, bf16[64,8192]{1,0:T(8,128)(2,1)} %tgt_ref.5, f32[1,8192]{1,0:T(1,128)} %bitcast.95, f32[1,8192]{1,0:T(1,128)} %reshape.111.tpot_ref), custom_call_target="tpu_custom_call" | custom-call | tf_op jit(solution)/shard_map/pallas_call | solution.py:244
  12.7 1.7 %collective-permute-start = (f32[2,2048]{1,0:T(2,128)S(1)}, f32[2,2048]{1,0:T(2,128)S(1)}, u32[]{:S(2)}, u32[]{:S(2)}) collective-permute-start(f32[2,2048]{1,0:T(2,128)S(1)} %pad_maximum_fusion.7), channel_id=1, source_target_pairs={{0,1},{1,0},{2,3},{3,2},{4,5},{5,4},{6,7},{7,6},{8,9},{9,8},{10,11... | collective-permute-start | bytes 49160 | tf_op jit(solution)/shard_map/ppermute | solution.py:31
  16.0 2.4 %collective-permute-start.1 = (f32[2,2048]{1,0:T(2,128)S(1)}, f32[2,2048]{1,0:T(2,128)S(1)}, u32[]{:S(2)}, u32[]{:S(2)}) collective-permute-start(f32[2,2048]{1,0:T(2,128)S(1)} %pad_maximum_fusion.8), channel_id=1, source_target_pairs={{0,2},{1,3},{2,0},{3,1},{4,6},{5,7},{6,4},{7,5},{8,10},{9,11},{10,... | collective-permute-start | bytes 49160 | tf_op jit(solution)/shard_map/ppermute | solution.py:31
  20.8 6.8 %shard_map.95 = (f32[1,8192]{1,0:T(1,128)}, f32[1,8192]{1,0:T(1,128)}) custom-call(s32[8,8]{1,0:T(8,128)} %blocks_ref.9, s32[8]{0:T(128)} %bitcast.137, bf16[64,2048]{1,0:T(8,128)(2,1)} %src_ref.9, f32[1,2048]{1,0:T(1,128)} %bitcast.125, bf16[80,8192]{1,0:T(8,128)(2,1)} %pad_maximum_fusion.tgt_ref, f32[1,8192]{1,0:T(1,128)} %bitcast.96), custom_call_target="tpu_custom_call" | custom-call | tf_op jit(solution)/shard_map/pallas_call | solution.py:244
  28.4 1.7 %collective-permute-start.2 = (f32[2,8192]{1,0:T(2,128)S(1)}, f32[2,8192]{1,0:T(2,128)S(1)}, u32[]{:S(2)}, u32[]{:S(2)}) collective-permute-start(f32[2,8192]{1,0:T(2,128)S(1)} %pad_maximum_fusion.1), channel_id=1, source_target_pairs={{0,4},{4,0},{8,12},{12,8},{16,20},{20,16},{24,28},{28,24},{1,5},{5... | collective-permute-start | bytes 196616 | tf_op jit(solution)/shard_map/ppermute | solution.py:31
  30.1 2.9 %collective-permute-done.2 = f32[2,8192]{1,0:T(2,128)S(1)} collective-permute-done((f32[2,8192]{1,0:T(2,128)S(1)}, f32[2,8192]{1,0:T(2,128)S(1)}, u32[]{:S(2)}, u32[]{:S(2)}) %collective-permute-start.2) | collective-permute-done | bytes 65568 | tf_op jit(solution)/shard_map/ppermute | solution.py:31
  34.0 2.9 %collective-permute-start.3 = (f32[2,8192]{1,0:T(2,128)S(1)}, f32[2,8192]{1,0:T(2,128)S(1)}, u32[]{:S(2)}, u32[]{:S(2)}) collective-permute-start(f32[2,8192]{1,0:T(2,128)S(1)} %pad_maximum_fusion.2), channel_id=1, source_target_pairs={{0,8},{4,12},{8,0},{12,4},{16,24},{20,28},{24,16},{28,20},{1,9},{5... | collective-permute-start | bytes 196616 | tf_op jit(solution)/shard_map/ppermute | solution.py:31
  36.8 2.2 %collective-permute-done.3 = f32[2,8192]{1,0:T(2,128)S(1)} collective-permute-done((f32[2,8192]{1,0:T(2,128)S(1)}, f32[2,8192]{1,0:T(2,128)S(1)}, u32[]{:S(2)}, u32[]{:S(2)}) %collective-permute-start.3) | collective-permute-done | bytes 65568 | tf_op jit(solution)/shard_map/ppermute | solution.py:31
  39.3 3.5 %collective-permute-start.4 = (f32[2,8192]{1,0:T(2,128)S(1)}, f32[2,8192]{1,0:T(2,128)S(1)}, u32[]{:S(2)}, u32[]{:S(2)}) collective-permute-start(f32[2,8192]{1,0:T(2,128)S(1)} %pad_maximum_fusion.3), channel_id=1, source_target_pairs={{0,16},{4,20},{8,24},{12,28},{16,0},{20,4},{24,8},{28,12},{1,17},{... | collective-permute-start | bytes 196616 | tf_op jit(solution)/shard_map/ppermute | solution.py:31
  42.8 2.2 %collective-permute-done.4 = f32[2,8192]{1,0:T(2,128)S(1)} collective-permute-done((f32[2,8192]{1,0:T(2,128)S(1)}, f32[2,8192]{1,0:T(2,128)S(1)}, u32[]{:S(2)}, u32[]{:S(2)}) %collective-permute-start.4) | collective-permute-done | bytes 65568 | tf_op jit(solution)/shard_map/ppermute | solution.py:31
  46.6 8.5 %shard_map.96 = (f32[1,2048]{1,0:T(1,128)}, f32[1,2048]{1,0:T(1,128)}) custom-call(s32[8,8]{1,0:T(8,128)} %blocks_ref.9, s32[8]{0:T(128)} %bitcast.138, bf16[64,2048]{1,0:T(8,128)(2,1)} %src_ref.9, bf16[64,8192]{1,0:T(8,128)(2,1)} %tgt_ref.5, f32[1,8192]{1,0:T(1,128)} %bitcast.97, f32[1,8192]{1,0:T(1,128)} %bitcast.107), custom_call_target="tpu_custom_call" | custom-call | tf_op jit(solution)/shard_map/pallas_call | solution.py:244
  57.8 3.2 %collective-permute-start.6 = (f32[2,2048]{1,0:T(2,128)S(1)}, f32[2,2048]{1,0:T(2,128)S(1)}, u32[]{:S(2)}, u32[]{:S(2)}) collective-permute-start(f32[2,2048]{1,0:T(2,128)S(1)} %pad_maximum_fusion.10), channel_id=1, source_target_pairs={{0,2},{1,3},{2,0},{3,1},{4,6},{5,7},{6,4},{7,5},{8,10},{9,11},{10,... | collective-permute-start | bytes 49160 | tf_op jit(solution)/shard_map/ppermute | solution.py:31
  61.0 1.7 %collective-permute-done.6 = f32[2,2048]{1,0:T(2,128)S(1)} collective-permute-done((f32[2,2048]{1,0:T(2,128)S(1)}, f32[2,2048]{1,0:T(2,128)S(1)}, u32[]{:S(2)}, u32[]{:S(2)}) %collective-permute-start.6) | collective-permute-done | bytes 16416 | tf_op jit(solution)/shard_map/ppermute | solution.py:31
  64.1 6.8 %shard_map.97 = (f32[1,8192]{1,0:T(1,128)}, f32[1,8192]{1,0:T(1,128)}) custom-call(s32[8,8]{1,0:T(8,128)} %blocks_ref.9, s32[8]{0:T(128)} %bitcast.139, bf16[64,2048]{1,0:T(8,128)(2,1)} %src_ref.9, f32[1,2048]{1,0:T(1,128)} %bitcast.124, bf16[80,8192]{1,0:T(8,128)(2,1)} %pad_maximum_fusion.tgt_ref, f32[1,8192]{1,0:T(1,128)} %bitcast.98), custom_call_target="tpu_custom_call" | custom-call | tf_op jit(solution)/shard_map/pallas_call | solution.py:244
  72.4 3.6 %collective-permute-done.7 = f32[2,8192]{1,0:T(2,128)S(1)} collective-permute-done((f32[2,8192]{1,0:T(2,128)S(1)}, f32[2,8192]{1,0:T(2,128)S(1)}, u32[]{:S(2)}, u32[]{:S(2)}) %collective-permute-start.7) | collective-permute-done | bytes 65568 | tf_op jit(solution)/shard_map/ppermute | solution.py:31
  77.0 2.5 %collective-permute-start.8 = (f32[2,8192]{1,0:T(2,128)S(1)}, f32[2,8192]{1,0:T(2,128)S(1)}, u32[]{:S(2)}, u32[]{:S(2)}) collective-permute-start(f32[2,8192]{1,0:T(2,128)S(1)} %pad_maximum_fusion.5), channel_id=1, source_target_pairs={{0,8},{4,12},{8,0},{12,4},{16,24},{20,28},{24,16},{28,20},{1,9},{5... | collective-permute-start | bytes 196616 | tf_op jit(solution)/shard_map/ppermute | solution.py:31
  79.5 2.2 %collective-permute-done.8 = f32[2,8192]{1,0:T(2,128)S(1)} collective-permute-done((f32[2,8192]{1,0:T(2,128)S(1)}, f32[2,8192]{1,0:T(2,128)S(1)}, u32[]{:S(2)}, u32[]{:S(2)}) %collective-permute-start.8) | collective-permute-done | bytes 65568 | tf_op jit(solution)/shard_map/ppermute | solution.py:31
  82.0 3.1 %collective-permute-start.9 = (f32[2,8192]{1,0:T(2,128)S(1)}, f32[2,8192]{1,0:T(2,128)S(1)}, u32[]{:S(2)}, u32[]{:S(2)}) collective-permute-start(f32[2,8192]{1,0:T(2,128)S(1)} %pad_maximum_fusion.6), channel_id=1, source_target_pairs={{0,16},{4,20},{8,24},{12,28},{16,0},{20,4},{24,8},{28,12},{1,17},{... | collective-permute-start | bytes 196616 | tf_op jit(solution)/shard_map/ppermute | solution.py:31
  85.1 2.2 %collective-permute-done.9 = f32[2,8192]{1,0:T(2,128)S(1)} collective-permute-done((f32[2,8192]{1,0:T(2,128)S(1)}, f32[2,8192]{1,0:T(2,128)S(1)}, u32[]{:S(2)}, u32[]{:S(2)}) %collective-permute-start.9) | collective-permute-done | bytes 65568 | tf_op jit(solution)/shard_map/ppermute | solution.py:31
  87.4 1.5 %multiply_subtract_fusion = f32[8192]{0:T(1024)} fusion(f32[8192]{0:T(1024)S(1)} %bitcast.111, f32[8192]{0:T(1024)S(1)} %bitcast.110, f32[8192]{0:T(1024)S(1)} %bitcast.115, f32[8192]{0:T(1024)S(1)} %bitcast.114, f32[8192]{0:T(1024)S(1)} %bitcast.113, f32[8192]{0:T(1024)S(1)} %bitcast.112, f32[8192]{0:T(1024)} %bitcast.102, f32[8192]{0:T(1024)} %bitcast.103, ...), kind=kLoop, calls=%fused_computation.12 | loop fusion | flops 180224 | bytes 327680 | tf_op jit(solution)/shard_map/sub | solution.py:303
  88.8 11.3 %shard_map.98 = (f32[1,2048]{1,0:T(1,128)}, f32[2048,128]{1,0:T(8,128)}, f32[1,2048]{1,0:T(1,128)}) custom-call(s32[8,8]{1,0:T(8,128)} %blocks_ref.9, s32[8]{0:T(128)} %bitcast.140, bf16[64,2048]{1,0:T(8,128)(2,1)} %src_ref.9, bf16[64,8192]{1,0:T(8,128)(2,1)} %tgt_ref.5, f32[1,8192]{1,0:T(1,128)} %bitcast.99, f32[1,8192]{1,0:T(1,128)} %bitcast.106, ...), custom_call_target="tpu_custom_call" | custom-call | tf_op jit(solution)/shard_map/pallas_call | solution.py:244
  108.3 4.7 %collective-permute-start.13 = (f32[1,512,128]{2,1,0:T(8,128)S(1)}, f32[1,512,128]{2,1,0:T(8,128)S(1)}, u32[]{:S(2)}, u32[]{:S(2)}) collective-permute-start(f32[1,512,128]{2,1,0:T(8,128)S(1)} %constant_dynamic-slice_fusion.1), channel_id=1, source_target_pairs={{0,2},{1,3},{2,0},{3,1},{4,6},{5,7},{6,4},{7,5},{8,10},{9,11},{10,... | collective-permute-start | bytes 786440 | tf_op jit(solution)/shard_map/ppermute | solution.py:61
  113.1 6.6 %collective-permute-done.12 = f32[2,1,512]{2,1,0:T(1,128)S(1)} collective-permute-done((f32[2,1,512]{2,1,0:T(1,128)S(1)}, f32[2,1,512]{2,1,0:T(1,128)S(1)}, u32[]{:S(2)}, u32[]{:S(2)}) %collective-permute-start.12) | collective-permute-done | bytes 4128 | tf_op jit(solution)/shard_map/ppermute | solution.py:60
  (66 shorter events, 25.0 us)
Async XLA Ops:
  0.6 17.8 %copy-start = (bf16[64,8192]{1,0:T(8,128)(2,1)S(1)}, bf16[64,8192]{1,0:T(8,128)(2,1)}, u32[]{:S(2)}) copy-start(bf16[64,8192]{1,0:T(8,128)(2,1)} %tgt_ref.5) | copy-start | bytes 3145732
  2.8 17.3 %copy-start.4 = (f32[2048]{0:T(1024)S(1)}, f32[2048]{0:T(1024)}, u32[]{:S(2)}) copy-start(f32[2048]{0:T(1024)} %param.10) | copy-start | bytes 24580
  11.9 8.2 %copy-start.2 = (f32[1,2048]{1,0:T(1,128)S(1)}, f32[1,2048]{1,0:T(1,128)}, u32[]{:S(2)}) copy-start(f32[1,2048]{1,0:T(1,128)} %get-tuple-element.14) | copy-start | bytes 24580
  11.9 8.2 %copy-start.3 = (f32[1,2048]{1,0:T(1,128)S(1)}, f32[1,2048]{1,0:T(1,128)}, u32[]{:S(2)}) copy-start(f32[1,2048]{1,0:T(1,128)} %get-tuple-element.15) | copy-start | bytes 24580
  12.7 2.5 %collective-permute-start = (f32[2,2048]{1,0:T(2,128)S(1)}, f32[2,2048]{1,0:T(2,128)S(1)}, u32[]{:S(2)}, u32[]{:S(2)}) collective-permute-start(f32[2,2048]{1,0:T(2,128)S(1)} %pad_maximum_fusion.7), channel_id=1, source_target_pairs={{0,1},{1,0},{2,3},{3,2},{4,5},{5,4},{6,7},{7,6},{8,9},{9,8},{10,11... | collective-permute-start | bytes 49160 | tf_op jit(solution)/shard_map/ppermute | solution.py:31
  16.0 29.1 %copy-start.1 = (f32[8192]{0:T(1024)S(1)}, f32[8192]{0:T(1024)}, u32[]{:S(2)}) copy-start(f32[8192]{0:T(1024)} %param.11) | copy-start | bytes 98308
  16.0 4.1 %collective-permute-start.1 = (f32[2,2048]{1,0:T(2,128)S(1)}, f32[2,2048]{1,0:T(2,128)S(1)}, u32[]{:S(2)}, u32[]{:S(2)}) collective-permute-start(f32[2,2048]{1,0:T(2,128)S(1)} %pad_maximum_fusion.8), channel_id=1, source_target_pairs={{0,2},{1,3},{2,0},{3,1},{4,6},{5,7},{6,4},{7,5},{8,10},{9,11},{10,... | collective-permute-start | bytes 49160 | tf_op jit(solution)/shard_map/ppermute | solution.py:31
  28.4 4.6 %collective-permute-start.2 = (f32[2,8192]{1,0:T(2,128)S(1)}, f32[2,8192]{1,0:T(2,128)S(1)}, u32[]{:S(2)}, u32[]{:S(2)}) collective-permute-start(f32[2,8192]{1,0:T(2,128)S(1)} %pad_maximum_fusion.1), channel_id=1, source_target_pairs={{0,4},{4,0},{8,12},{12,8},{16,20},{20,16},{24,28},{28,24},{1,5},{5... | collective-permute-start | bytes 196616 | tf_op jit(solution)/shard_map/ppermute | solution.py:31
  34.0 5.1 %collective-permute-start.3 = (f32[2,8192]{1,0:T(2,128)S(1)}, f32[2,8192]{1,0:T(2,128)S(1)}, u32[]{:S(2)}, u32[]{:S(2)}) collective-permute-start(f32[2,8192]{1,0:T(2,128)S(1)} %pad_maximum_fusion.2), channel_id=1, source_target_pairs={{0,8},{4,12},{8,0},{12,4},{16,24},{20,28},{24,16},{28,20},{1,9},{5... | collective-permute-start | bytes 196616 | tf_op jit(solution)/shard_map/ppermute | solution.py:31
  39.3 5.8 %collective-permute-start.4 = (f32[2,8192]{1,0:T(2,128)S(1)}, f32[2,8192]{1,0:T(2,128)S(1)}, u32[]{:S(2)}, u32[]{:S(2)}) collective-permute-start(f32[2,8192]{1,0:T(2,128)S(1)} %pad_maximum_fusion.3), channel_id=1, source_target_pairs={{0,16},{4,20},{8,24},{12,28},{16,0},{20,4},{24,8},{28,12},{1,17},{... | collective-permute-start | bytes 196616 | tf_op jit(solution)/shard_map/ppermute | solution.py:31
  55.8 1.2 %collective-permute-start.5 = (f32[2,2048]{1,0:T(2,128)S(1)}, f32[2,2048]{1,0:T(2,128)S(1)}, u32[]{:S(2)}, u32[]{:S(2)}) collective-permute-start(f32[2,2048]{1,0:T(2,128)S(1)} %pad_maximum_fusion.9), channel_id=1, source_target_pairs={{0,1},{1,0},{2,3},{3,2},{4,5},{5,4},{6,7},{7,6},{8,9},{9,8},{10,11... | collective-permute-start | bytes 49160 | tf_op jit(solution)/shard_map/ppermute | solution.py:31
  57.8 4.9 %collective-permute-start.6 = (f32[2,2048]{1,0:T(2,128)S(1)}, f32[2,2048]{1,0:T(2,128)S(1)}, u32[]{:S(2)}, u32[]{:S(2)}) collective-permute-start(f32[2,2048]{1,0:T(2,128)S(1)} %pad_maximum_fusion.10), channel_id=1, source_target_pairs={{0,2},{1,3},{2,0},{3,1},{4,6},{5,7},{6,4},{7,5},{8,10},{9,11},{10,... | collective-permute-start | bytes 49160 | tf_op jit(solution)/shard_map/ppermute | solution.py:31
  71.7 4.3 %collective-permute-start.7 = (f32[2,8192]{1,0:T(2,128)S(1)}, f32[2,8192]{1,0:T(2,128)S(1)}, u32[]{:S(2)}, u32[]{:S(2)}) collective-permute-start(f32[2,8192]{1,0:T(2,128)S(1)} %pad_maximum_fusion.4), channel_id=1, source_target_pairs={{0,4},{4,0},{8,12},{12,8},{16,20},{20,16},{24,28},{28,24},{1,5},{5... | collective-permute-start | bytes 196616 | tf_op jit(solution)/shard_map/ppermute | solution.py:31
  77.0 4.8 %collective-permute-start.8 = (f32[2,8192]{1,0:T(2,128)S(1)}, f32[2,8192]{1,0:T(2,128)S(1)}, u32[]{:S(2)}, u32[]{:S(2)}) collective-permute-start(f32[2,8192]{1,0:T(2,128)S(1)} %pad_maximum_fusion.5), channel_id=1, source_target_pairs={{0,8},{4,12},{8,0},{12,4},{16,24},{20,28},{24,16},{28,20},{1,9},{5... | collective-permute-start | bytes 196616 | tf_op jit(solution)/shard_map/ppermute | solution.py:31
  82.0 5.3 %collective-permute-start.9 = (f32[2,8192]{1,0:T(2,128)S(1)}, f32[2,8192]{1,0:T(2,128)S(1)}, u32[]{:S(2)}, u32[]{:S(2)}) collective-permute-start(f32[2,8192]{1,0:T(2,128)S(1)} %pad_maximum_fusion.6), channel_id=1, source_target_pairs={{0,16},{4,20},{8,24},{12,28},{16,0},{20,4},{24,8},{28,12},{1,17},{... | collective-permute-start | bytes 196616 | tf_op jit(solution)/shard_map/ppermute | solution.py:31
  104.5 2.3 %collective-permute-start.11 = (f32[2,512,128]{2,1,0:T(8,128)S(1)}, f32[2,512,128]{2,1,0:T(8,128)S(1)}, u32[]{:S(2)}, u32[]{:S(2)}) collective-permute-start(f32[2,512,128]{2,1,0:T(8,128)S(1)} %dynamic-slice_bitcast_fusion), channel_id=1, source_target_pairs={{0,1},{1,0},{2,3},{3,2},{4,5},{5,4},{6,7},{7,6},{8,9},{9,8},{10,11... | collective-permute-start | bytes 1572872 | tf_op jit(solution)/shard_map/ppermute | solution.py:61
  105.3 1.5 %collective-permute-start.10 = (f32[2,2,512]{2,1,0:T(2,128)S(1)}, f32[2,2,512]{2,1,0:T(2,128)S(1)}, u32[]{:S(2)}, u32[]{:S(2)}) collective-permute-start(f32[2,2,512]{2,1,0:T(2,128)S(1)} %pad_maximum_fusion.11), channel_id=1, source_target_pairs={{0,1},{1,0},{2,3},{3,2},{4,5},{5,4},{6,7},{7,6},{8,9},{9,8},{10,11... | collective-permute-start | bytes 24584 | tf_op jit(solution)/shard_map/ppermute | solution.py:60
  108.3 11.5 %collective-permute-start.13 = (f32[1,512,128]{2,1,0:T(8,128)S(1)}, f32[1,512,128]{2,1,0:T(8,128)S(1)}, u32[]{:S(2)}, u32[]{:S(2)}) collective-permute-start(f32[1,512,128]{2,1,0:T(8,128)S(1)} %constant_dynamic-slice_fusion.1), channel_id=1, source_target_pairs={{0,2},{1,3},{2,0},{3,1},{4,6},{5,7},{6,4},{7,5},{8,10},{9,11},{10,... | collective-permute-start | bytes 786440 | tf_op jit(solution)/shard_map/ppermute | solution.py:61
  113.1 6.7 %collective-permute-start.12 = (f32[2,1,512]{2,1,0:T(1,128)S(1)}, f32[2,1,512]{2,1,0:T(1,128)S(1)}, u32[]{:S(2)}, u32[]{:S(2)}) collective-permute-start(f32[2,1,512]{2,1,0:T(1,128)S(1)} %pad_maximum_fusion.12), channel_id=1, source_target_pairs={{0,2},{1,3},{2,0},{3,1},{4,6},{5,7},{6,4},{7,5},{8,10},{9,11},{10,... | collective-permute-start | bytes 12296 | tf_op jit(solution)/shard_map/ppermute | solution.py:60
